TPU v7x, 512 devices: a whole 4x8x8 slice. The times are simulated.
512 devices in a mesh: ens: 16 (over z, x_hi), tile: 32 (over y, x_lo, core).
Axes of the slice: x: 4 (x_hi: 2, x_lo: 2; x = x_hi * 2 + x_lo), y: 8, z: 8, core: 2. Of those that a mesh axis runs over, the one named last changes fastest.
Arguments:
- conditioning: bfloat16 [12, 256, 128], P(None, 'tile'), may hold values from -6 to 6
- member_noise: float32 [16, 4, 256, 128], P('ens', None, 'tile'), may hold values from -6 to 6
- reg_in: bfloat16 [3, 3, 12, 128], replicated, may hold values from -1 to 1
- reg_down: bfloat16 [3, 3, 128, 128], replicated, may hold values from -0.25 to 0.25
- reg_low: bfloat16 [3, 3, 128, 128], replicated, may hold values from -0.25 to 0.25
- reg_up: bfloat16 [4, 4, 128, 128], replicated, may hold values from -0.375 to 0.375
- reg_fine: bfloat16 [3, 3, 128, 128], replicated, may hold values from -0.25 to 0.25
- reg_out: bfloat16 [3, 3, 4, 128], replicated, may hold values from -0.3125 to 0.3125
- dif_in: bfloat16 [3, 3, 20, 128], replicated, may hold values from -0.75 to 0.75
- dif_down: bfloat16 [3, 3, 128, 128], replicated, may hold values from -0.25 to 0.25
- dif_low: bfloat16 [3, 3, 128, 128], replicated, may hold values from -0.25 to 0.25
- dif_up: bfloat16 [4, 4, 128, 128], replicated, may hold values from -0.375 to 0.375
- dif_fine: bfloat16 [3, 3, 128, 128], replicated, may hold values from -0.25 to 0.25
- dif_out: bfloat16 [3, 3, 4, 128], replicated, may hold values from -0.3125 to 0.3125
Outputs:
- prediction: float32 [16, 4, 256, 128], P('ens', None, 'tile')
All inputs are finite; a program needn't handle non-finite values.
Results may differ from a plain program's by a relative error of at most 0.015.
Values may be sent and summed in bfloat16 or wider, within the bound.
No kernel may reach another device: no remote copies, remote signals or barrier semaphores. Data moves between devices by JAX's collectives and lax.ppermute only.
A program may use at most 64 MiB of HBM per device.

v0:
```python
import jax
import jax.numpy as jnp
from jax import lax
from jax.sharding import PartitionSpec as P

STEPS = 2


sigma_top = 1.0
sigma_ratio = 0.4
sigma_data = 0.5


def from_tile(values, distance):
    count = lax.axis_size("tile")
    pairs = [(i + distance, i) for i in range(count) if 0 <= i + distance < count]
    return lax.ppermute(values, "tile", pairs)


def halo_rows(values, dim, below, above):
    rows = values.shape[dim]
    pieces = []
    need = below
    distance = 1
    while need > 0:
        take = min(need, rows)
        part = lax.slice_in_dim(values, rows - take, rows, axis=dim)
        pieces.insert(0, from_tile(part, -distance))
        need -= take
        distance += 1
    pieces.append(values)
    need = above
    distance = 1
    while need > 0:
        take = min(need, rows)
        part = lax.slice_in_dim(values, 0, take, axis=dim)
        pieces.append(from_tile(part, distance))
        need -= take
        distance += 1
    return jnp.concatenate(pieces, axis=dim)


def row_mask(values, first, base, limit, axis=0):
    shape = [1] * values.ndim
    shape[axis] = values.shape[axis]
    index = base + first + lax.broadcasted_iota(jnp.int32, tuple(shape), axis)
    keep = (index >= 0) & (index < limit)
    return jnp.where(keep, values, jnp.zeros_like(values))


def conv(lhs, rhs, specs, strides=(1, 1), padding=((0, 0), (1, 1)), dilation=(1, 1)):
    return lax.conv_general_dilated(
        lhs,
        rhs,
        window_strides=strides,
        padding=padding,
        lhs_dilation=dilation,
        dimension_numbers=specs,
        preferred_element_type=jnp.float32,
    )


def silu(values):
    return jax.nn.silu(values)


def windows(out_lo, out_hi):
    join_lo, join_hi = out_lo - 2, out_hi + 2
    mid_lo, mid_hi = join_lo // 2 - 1, join_hi // 2 + 1
    crs_lo, crs_hi = mid_lo - 1, mid_hi + 1
    top_lo, top_hi = min(2 * crs_lo - 1, join_lo), max(2 * crs_hi, join_hi)
    return join_lo, join_hi, mid_lo, mid_hi, crs_lo, crs_hi, top_lo, top_hi


def conv_in(fields, first, out_lo, out_hi, weight):
    count, _, cols = fields.shape
    lo, hi = out_lo - 1 - first, out_hi + 1 - first
    assert lo >= 0 and hi <= fields.shape[1]
    padded = jnp.pad(fields[:, lo:hi], ((0, 0), (0, 0), (1, 1)))
    rows = out_hi - out_lo
    patches = jnp.concatenate(
        [padded[:, ty : ty + rows, tx : tx + cols] for ty in range(3) for tx in range(3)], axis=0
    )
    flat = weight.reshape(9 * count, weight.shape[3])
    return jnp.einsum("krw,ko->rwo", patches, flat, preferred_element_type=jnp.float32)


def unet(fields, first, out_lo, out_hi, weights, base, grid_rows, top_extra=None):
    w_in, w_down, w_low, w_up, w_fine, w_out = weights
    join_lo, join_hi, mid_lo, mid_hi, crs_lo, crs_hi, top_lo, top_hi = windows(out_lo, out_hi)
    top = conv_in(fields, first, top_lo, top_hi, w_in[:, :, : fields.shape[0]])
    if top_extra is not None:
        top = top + top_extra
    top = row_mask(silu(top), top_lo, base, grid_rows).astype(jnp.bfloat16)
    down_in = top[2 * crs_lo - 1 - top_lo : 2 * crs_hi - top_lo][None]
    coarse = conv(down_in, w_down, ("NHWC", "HWIO", "NHWC"), strides=(2, 2))[0]
    coarse = row_mask(silu(coarse), crs_lo, base // 2, grid_rows // 2).astype(jnp.bfloat16)
    middle = conv(coarse[None], w_low, ("NHWC", "HWIO", "NHWC"))[0]
    middle = row_mask(silu(middle), mid_lo, base // 2, grid_rows // 2).astype(jnp.bfloat16)
    upward = conv(
        middle[None],
        w_up[::-1, ::-1],
        ("NHWC", "HWIO", "NHWC"),
        padding=((0, 0), (2, 2)),
        dilation=(2, 2),
    )[0]
    joined = top[join_lo - top_lo : join_hi - top_lo].astype(jnp.float32) + upward
    joined = row_mask(joined, join_lo, base, grid_rows).astype(jnp.bfloat16)
    refined = conv(joined[None], w_fine, ("NHWC", "HWIO", "NHWC"))[0]
    refined = row_mask(silu(refined), join_lo + 1, base, grid_rows).astype(jnp.bfloat16)
    out_count = w_out.shape[2]
    lanes = w_out.shape[3]
    w_wide = jnp.pad(w_out, ((0, 0), (0, 0), (0, lanes - out_count), (0, 0)))
    result = conv(refined[None], w_wide, ("NHWC", "HWOI", "NHWC"))[0]
    return jnp.transpose(result[..., :out_count], (2, 0, 1))


def shards(
    conditioning,
    member_noise,
    reg_in,
    reg_down,
    reg_low,
    reg_up,
    reg_fine,
    reg_out,
    dif_in,
    dif_down,
    dif_low,
    dif_up,
    dif_fine,
    dif_out,
):
    rows = conditioning.shape[1]
    grid_rows = rows * lax.axis_size("tile")
    base = lax.axis_index("tile") * rows
    reg_weights = (reg_in, reg_down, reg_low, reg_up, reg_fine, reg_out)
    dif_weights = (dif_in, dif_down, dif_low, dif_up, dif_fine, dif_out)
    cond_count = conditioning.shape[0]
    noise_count = member_noise.shape[1]

    residual_field = sigma_top * member_noise[0]
    gains = []
    for step_index in range(STEPS):
        sigma_now = sigma_top * sigma_ratio**step_index
        sigma_next = sigma_top * sigma_ratio ** (step_index + 1) if step_index + 1 < STEPS else 0.0
        scale_sq = sigma_now**2 + sigma_data**2
        gains.append(
            (
                1.0 / scale_sq**0.5,
                sigma_data**2 / scale_sq,
                sigma_now * sigma_data / scale_sq**0.5,
                (sigma_next - sigma_now) / sigma_now,
            )
        )

    dif_halo = 8
    reg_halo = 2 * dif_halo
    noise_in = (gains[0][0] * residual_field).astype(jnp.bfloat16)
    near = jnp.concatenate([noise_in, conditioning], axis=0)
    if rows == dif_halo:
        near_below = from_tile(near, -1)
        near_above = from_tile(near, 1)
        near_wide = jnp.concatenate([near_below, near, near_above], axis=1)
        cond_wide = jnp.concatenate(
            [
                from_tile(conditioning, -2),
                near_wide[noise_count:],
                from_tile(conditioning, 2),
            ],
            axis=1,
        )
    else:
        near_wide = halo_rows(near, 1, dif_halo, dif_halo)
        cond_wide = halo_rows(conditioning, 1, reg_halo, reg_halo)

    mean_wide = unet(cond_wide, -reg_halo, -dif_halo, rows + dif_halo, reg_weights, base, grid_rows)
    mean_wide = row_mask(mean_wide, -dif_halo, base, grid_rows, axis=1)
    mean_input = mean_wide.astype(jnp.bfloat16)
    cond_near = near_wide[noise_count:]
    reg_mean = mean_wide[:, dif_halo : dif_halo + rows]

    dif_top_lo, dif_top_hi = windows(0, rows)[6:]
    fixed_in = jnp.concatenate([cond_near, mean_input], axis=0)
    fixed_top = conv_in(
        fixed_in, -dif_halo, dif_top_lo, dif_top_hi, dif_in[:, :, noise_count:]
    )
    field_in = near_wide[:noise_count]
    for step_index in range(STEPS):
        in_gain, skip_gain, out_gain, step_gain = gains[step_index]
        if step_index > 0:
            field_in = halo_rows(
                (in_gain * residual_field).astype(jnp.bfloat16), 1, dif_halo, dif_halo
            )
        network = unet(
            field_in, -dif_halo, 0, rows, dif_weights, base, grid_rows, top_extra=fixed_top
        )
        denoised = skip_gain * residual_field + out_gain * network
        residual_field = residual_field + step_gain * (residual_field - denoised)
    return (reg_mean + residual_field)[None]


def solution(mesh):
    return jax.shard_map(
        shards,
        mesh=mesh,
        in_specs=(
            P(None, "tile", None),
            P("ens", None, "tile", None),
            P(),
            P(),
            P(),
            P(),
            P(),
            P(),
            P(),
            P(),
            P(),
            P(),
            P(),
            P(),
        ),
        out_specs=P("ens", None, "tile", None),
        check_vma=False,
    )
```

profile of v0, /device:TPU:415, one launch (start us, length us, event | category | flops | bytes accessed | tf_op | source)
XLA Modules:
  0.0 74.2 jit_solution(4525196958062072961)
XLA Ops:
  0.0 0.8 %copy.38 = bf16[12,8,128]{2,0,1:T(8,128)(2,1)S(1)} copy(bf16[12,8,128]{2,1,0:T(8,128)(2,1)} %param.14) | data formatting | bytes 49152 | tf_op args[0]
  0.8 0.7 fusion.257
  1.6 5.2 %collective-permute-start.1 = (bf16[16,8,128]{2,0,1:T(8,128)(2,1)S(1)}, bf16[16,8,128]{2,0,1:T(8,128)(2,1)S(1)}, u32[]{:S(2)}, u32[]{:S(2)}) collective-permute-start(bf16[16,8,128]{2,0,1:T(8,128)(2,1)S(1)} %pad_maximum_fusion.3), channel_id=1, source_target_pairs={{0,1},{1,2},{2,3},{3,4},{4,5},{5,6},{6,7},{7,8},{8,9},{9,10},{10,1... | collective-permute-start | bytes 98312 | tf_op jit(solution)/shard_map/ppermute | solution.py:17
  6.8 1.9 %collective-permute-start.2 = (bf16[16,8,128]{2,0,1:T(8,128)(2,1)S(1)}, bf16[16,8,128]{2,0,1:T(8,128)(2,1)S(1)}, u32[]{:S(2)}, u32[]{:S(2)}) collective-permute-start(bf16[16,8,128]{2,0,1:T(8,128)(2,1)S(1)} %pad_maximum_fusion.3), channel_id=1, source_target_pairs={{1,0},{2,1},{3,2},{4,3},{5,4},{6,5},{7,6},{8,7},{9,8},{10,9},{11,1... | collective-permute-start | bytes 98312 | tf_op jit(solution)/shard_map/ppermute | solution.py:17
  8.7 2.8 %collective-permute-start = (bf16[12,8,128]{2,0,1:T(8,128)(2,1)S(1)}, bf16[12,8,128]{2,0,1:T(8,128)(2,1)S(1)}, u32[]{:S(2)}, u32[]{:S(2)}) collective-permute-start(bf16[12,8,128]{2,0,1:T(8,128)(2,1)S(1)} %copy.38), channel_id=1, source_target_pairs={{0,2},{1,3},{2,4},{3,5},{4,6},{5,7},{6,8},{7,9},{8,10},{9,11},{10,... | collective-permute-start | bytes 73736 | tf_op jit(solution)/shard_map/ppermute | solution.py:17
  11.6 2.5 %collective-permute-start.3 = (bf16[12,8,128]{2,0,1:T(8,128)(2,1)S(1)}, bf16[12,8,128]{2,0,1:T(8,128)(2,1)S(1)}, u32[]{:S(2)}, u32[]{:S(2)}) collective-permute-start(bf16[12,8,128]{2,0,1:T(8,128)(2,1)S(1)} %copy.38), channel_id=1, source_target_pairs={{2,0},{3,1},{4,2},{5,3},{6,4},{7,5},{8,6},{9,7},{10,8},{11,9},{12,... | collective-permute-start | bytes 73736 | tf_op jit(solution)/shard_map/ppermute | solution.py:17
  14.2 0.8 %slice.213 = bf16[3,3,16,128]{3,2,1,0:T(8,128)(2,1)S(1)} slice(bf16[3,3,20,128]{3,2,1,0:T(8,128)(2,1)} %param.22), slice={[0:3], [0:3], [4:20], [0:128]} | slice | bytes 73728 | tf_op jit(solution)/shard_map/slice | solution.py:186
  15.1 0.7 slice.202
  15.8 0.8 %reshape.269 = bf16[108,128,1]{1,0,2:T(8,128)(2,1)S(1)} reshape(bf16[3,3,12,128]{3,2,1,0:T(8,128)(2,1)} %param.16) | data formatting | bytes 55296 | tf_op jit(solution)/shard_map/reshape | solution.py:84
  16.7 1.6 %collective-permute-done.3 = bf16[12,8,128]{2,0,1:T(8,128)(2,1)S(1)} collective-permute-done((bf16[12,8,128]{2,0,1:T(8,128)(2,1)S(1)}, bf16[12,8,128]{2,0,1:T(8,128)(2,1)S(1)}, u32[]{:S(2)}, u32[]{:S(2)}) %collective-permute-start.3) | collective-permute-done | bytes 24608 | tf_op jit(solution)/shard_map/ppermute | solution.py:17
  18.4 0.3 pad_slice_fusion
  18.7 6.0 %concatenate.30 = bf16[108,37,128]{2,0,1:T(8,128)(2,1)S(1)} concatenate(bf16[12,37,128]{2,0,1:T(8,128)(2,1)S(1)} %get-tuple-element.29, bf16[12,37,128]{2,0,1:T(8,128)(2,1)S(1)} %get-tuple-element.52, bf16[12,37,128]{2,0,1:T(8,128)(2,1)S(1)} %get-tuple-element.25, bf16[12,37,128]{2,0,1:T(8,128)(2,1)S(1)} %get-tuple-element.26, bf16[12,37,128]{2,0,1:T(8,128)(2,1)S(1)} %get-tuple-element.53, ...), dimensions={0} | concatenate | bytes 2045952 | tf_op jit(solution)/shard_map/concatenate | solution.py:81
  24.7 1.0 %select_convert_fusion = bf16[37,128,128]{2,1,0:T(8,128)(2,1)S(1)} fusion(bf16[108,37,128]{2,0,1:T(8,128)(2,1)S(1)} %concatenate.30, bf16[108,128,1]{1,0,2:T(8,128)(2,1)S(1)} %reshape.269, pred[37]{0:T(512)(128)(4,1)S(1)} %compare_and_fusion.7), kind=kOutput, calls=%fused_computation.2 | convolution fusion | flops 134578176 | bytes 2263077 | tf_op jit(solution)/shard_map/krw,ko->rwo/dot_general | solution.py:85
  25.7 0.8 %copy.86 = bf16[37,1,128,128]{3,0,2,1:T(8,128)(2,1)S(1)} copy(bf16[37,1,128,128]{3,2,0,1:T(8,128)(2,1)S(1)} %bitcast.214) | data formatting | bytes 2424832
  26.5 0.2 pad.29.clone
  26.8 0.4 copy.44
  27.2 0.5 copy-done.4
  27.8 1.0 %fusion.71 = bf16[18,1,8,9,128]{4,2,3,0,1:T(8,128)(2,1)S(1)} fusion(bf16[3,3,128,128]{3,2,1,0:T(8,128)(2,1)S(1)} %copy-done.4, bf16[37,1,7,2,128]{4,2,3,0,1:T(8,128)(2,1)S(1)} %slice.267, bf16[37,1,8,18,128]{4,2,3,0,1:T(8,128)(2,1)S(1)} %copy.44, pred[18]{0:T(512)(128)(4,1)S(1)} %compare_and_fusion.5, pred[8,9]{0,1:T(8,128)(4,1)S(1)} %copy-done.15), kind=kOutput, calls=%fused_computation.85 | convolution fusion | flops 388079616 | bytes 2123354 | tf_op jit(solution)/shard_map/conv_general_dilated | solution.py:52
  28.8 0.9 %fusion.102 = bf16[16,8,9,128]{3,1,2,0:T(8,128)(2,1)S(1)} fusion(bf16[3,3,128,128]{3,2,1,0:T(8,128)(2,1)S(1)} %copy-done.5, bf16[18,1,7,1,128]{4,2,3,0,1:T(8,128)(2,1)S(1)} %get-tuple-element.14, bf16[18,1,7,1,128]{4,2,3,0,1:T(8,128)(2,1)S(1)} %get-tuple-element.13, bf16[18,1,8,9,128]{4,2,3,0,1:T(8,128)(2,1)S(1)} %fusion.71, ...), kind=kOutput, calls=%fused_computation.120 | convolution fusion | flops 342798336 | bytes 986200 | tf_op jit(solution)/shard_map/conv_general_dilated | solution.py:52
  30.0 1.1 %fusion.154 = f32[28,8,16,128]{3,1,2,0:T(8,128)S(1)} fusion(bf16[4,4,128,128]{3,2,1,0:T(8,128)(2,1)S(1)} %copy-done, bf16[16,1,7,1,128]{4,2,3,0,1:T(8,128)(2,1)S(1)} %get-tuple-element.16, bf16[16,1,7,1,128]{4,2,3,0,1:T(8,128)(2,1)S(1)} %get-tuple-element.15, bf16[16,1,8,8,128]{4,2,3,0,1:T(8,128)(2,1)S(1)} %copy.47), kind=kOutput, calls=%fused_computation.155 | convolution fusion | flops 471400448 | bytes 2678784 | tf_op jit(solution)/shard_map/conv_general_dilated | solution.py:52
  31.1 0.3 copy.50
  31.4 0.3 fusion.5
  31.7 0.6 copy.87
  32.4 0.2 pad.35.clone
  32.6 0.4 copy.53
  33.0 0.3 copy-done.6
  33.3 2.5 %fusion.19 = bf16[26,1,8,17,128]{4,2,3,0,1:T(8,128)(2,1)S(1)} fusion(bf16[3,3,128,128]{3,2,1,0:T(8,128)(2,1)S(1)} %copy-done.6, bf16[28,1,7,2,128]{4,2,3,0,1:T(8,128)(2,1)S(1)} %slice.273, bf16[28,1,8,17,128]{4,2,3,0,1:T(8,128)(2,1)S(1)} %copy.53, pred[26]{0:T(512)(128)(4,1)S(1)} %compare_and_fusion.9, pred[8,17]{0,1:T(8,128)(4,1)S(1)} %copy-done.14), kind=kOutput, calls=%fused_computation.30 | convolution fusion | flops 1049698304 | bytes 2275490 | tf_op jit(solution)/shard_map/conv_general_dilated | solution.py:52
  35.9 2.4 %fusion.28 = f32[24,8,17,128]{3,1,2,0:T(8,128)S(1)} fusion(bf16[26,1,7,1,128]{4,2,3,0,1:T(8,128)(2,1)S(1)} %get-tuple-element.8, bf16[26,1,7,1,128]{4,2,3,0,1:T(8,128)(2,1)S(1)} %get-tuple-element.7, bf16[26,1,8,17,128]{4,2,3,0,1:T(8,128)(2,1)S(1)} %fusion.19, bf16[3,3,4,128]{3,2,1,0:T(4,128)(2,1)S(1)} %copy-done.12), kind=kOutput, calls=%fused_computation.40 | convolution fusion | flops 967651328 | bytes 2678784 | tf_op jit(solution)/shard_map/conv_general_dilated | solution.py:52
  38.2 0.3 copy.54
  38.7 1.7 %copy.83 = f32[24,1,128,128]{2,3,0,1:T(8,128)} copy(f32[24,1,128,128]{3,0,2,1:T(8,128)S(1)} %slice.276) | data formatting | bytes 3145728
  40.3 1.0 %fusion.312 = (bf16[4,24,128]{2,0,1:T(4,128)(2,1)S(1)}, f32[4,24,128]{2,0,1:T(4,128)S(1)}) fusion(f32[24,128,128]{1,2,0:T(8,128)} %bitcast.222, pred[24]{0:T(512)(128)(4,1)S(1)} %compare_and_fusion.10), kind=kLoop, calls=%fused_computation.345 | loop fusion | flops 24576 | bytes 122904 | tf_op jit(solution)/shard_map/convert_element_type | solution.py:179
  42.3 0.6 fusion.326
  42.9 0.2 concatenate.31
  43.1 0.6 select_convert_fusion.3
  43.8 0.5 copy.88
  44.4 0.2 copy.58
  44.7 0.5 copy-done.7
  45.2 0.6 fusion.149
  45.9 0.3 copy-done.9
  46.2 0.5 fusion.177
  46.8 0.4 copy-done.2
  47.2 0.6 fusion.208
  48.4 0.6 copy-done.11
  49.0 1.1 %fusion.65 = bf16[10,1,8,17,128]{4,2,3,0,1:T(8,128)(2,1)S(1)} fusion(bf16[3,3,128,128]{3,2,1,0:T(8,128)(2,1)S(1)} %copy-done.11, bf16[12,1,7,2,128]{4,2,3,0,1:T(8,128)(2,1)S(1)} %slice.296, bf16[12,1,8,17,128]{4,2,3,0,1:T(8,128)(2,1)S(1)} %copy.66, pred[10]{0:T(512)(128)(4,1)S(1)} %compare_and_fusion.4, pred[8,17]{0,1:T(8,128)(4,1)S(1)} %copy-done.14), kind=kOutput, calls=%fused_computation.82 | convolution fusion | flops 403873792 | bytes 1104018 | tf_op jit(solution)/shard_map/conv_general_dilated | solution.py:52
  50.1 0.8 %fusion.114 = f32[8,8,17,128]{3,1,2,0:T(8,128)S(1)} fusion(bf16[3,3,4,128]{3,2,1,0:T(4,128)(2,1)S(1)} %copy-done.13, bf16[10,1,7,1,128]{4,2,3,0,1:T(8,128)(2,1)S(1)} %get-tuple-element.12, bf16[10,1,7,1,128]{4,2,3,0,1:T(8,128)(2,1)S(1)} %get-tuple-element.11, bf16[10,1,8,17,128]{4,2,3,0,1:T(8,128)(2,1)S(1)} %fusion.65), kind=kOutput, calls=%fused_computation.129 | convolution fusion | flops 322809856 | bytes 950272 | tf_op jit(solution)/shard_map/conv_general_dilated | solution.py:52
  51.1 0.2 copy.84
  51.3 0.3 copy-done.1
  51.7 6.8 %collective-permute-start.4 = (bf16[4,8,128]{2,0,1:T(4,128)(2,1)S(1)}, bf16[4,8,128]{2,0,1:T(4,128)(2,1)S(1)}, u32[]{:S(2)}, u32[]{:S(2)}) collective-permute-start(bf16[4,8,128]{2,0,1:T(4,128)(2,1)S(1)} %multiply_convert_fusion), channel_id=1, source_target_pairs={{0,1},{1,2},{2,3},{3,4},{4,5},{5,6},{6,7},{7,8},{8,9},{9,10},{10,1... | collective-permute-start | bytes 24584 | tf_op jit(solution)/shard_map/ppermute | solution.py:17
  58.5 2.1 %collective-permute-start.5 = (bf16[4,8,128]{2,0,1:T(4,128)(2,1)S(1)}, bf16[4,8,128]{2,0,1:T(4,128)(2,1)S(1)}, u32[]{:S(2)}, u32[]{:S(2)}) collective-permute-start(bf16[4,8,128]{2,0,1:T(4,128)(2,1)S(1)} %multiply_convert_fusion), channel_id=1, source_target_pairs={{1,0},{2,1},{3,2},{4,3},{5,4},{6,5},{7,6},{8,7},{9,8},{10,9},{11,1... | collective-permute-start | bytes 24584 | tf_op jit(solution)/shard_map/ppermute | solution.py:17
  60.7 4.9 %collective-permute-done.5 = bf16[4,8,128]{2,0,1:T(4,128)(2,1)S(1)} collective-permute-done((bf16[4,8,128]{2,0,1:T(4,128)(2,1)S(1)}, bf16[4,8,128]{2,0,1:T(4,128)(2,1)S(1)}, u32[]{:S(2)}, u32[]{:S(2)}) %collective-permute-start.5) | collective-permute-done | bytes 8224 | tf_op jit(solution)/shard_map/ppermute | solution.py:17
  65.8 0.2 concatenate.35
  66.0 0.6 select_convert_fusion.2
  66.7 0.5 copy.89
  67.3 0.2 copy.71
  67.5 0.5 copy-done.8
  68.1 0.6 fusion.141
  68.8 0.3 copy-done.10
  69.1 0.5 fusion.187
  69.7 0.4 copy-done.3
  70.1 0.6 fusion.213
  71.3 1.1 %fusion.63 = bf16[10,1,8,17,128]{4,2,3,0,1:T(8,128)(2,1)S(1)} fusion(bf16[3,3,128,128]{3,2,1,0:T(8,128)(2,1)S(1)} %copy-done.11, bf16[12,1,7,2,128]{4,2,3,0,1:T(8,128)(2,1)S(1)} %slice.312, bf16[12,1,8,17,128]{4,2,3,0,1:T(8,128)(2,1)S(1)} %copy.79, pred[10]{0:T(512)(128)(4,1)S(1)} %compare_and_fusion.4, pred[8,17]{0,1:T(8,128)(4,1)S(1)} %copy-done.14), kind=kOutput, calls=%fused_computation.79 | convolution fusion | flops 403873792 | bytes 1104018 | tf_op jit(solution)/shard_map/conv_general_dilated | solution.py:52
  72.4 0.8 %fusion.112 = f32[8,8,17,128]{3,1,2,0:T(8,128)S(1)} fusion(bf16[3,3,4,128]{3,2,1,0:T(4,128)(2,1)S(1)} %copy-done.13, bf16[10,1,7,1,128]{4,2,3,0,1:T(8,128)(2,1)S(1)} %get-tuple-element.10, bf16[10,1,7,1,128]{4,2,3,0,1:T(8,128)(2,1)S(1)} %get-tuple-element.9, bf16[10,1,8,17,128]{4,2,3,0,1:T(8,128)(2,1)S(1)} %fusion.63), kind=kOutput, calls=%fused_computation.127 | convolution fusion | flops 322809856 | bytes 950272 | tf_op jit(solution)/shard_map/conv_general_dilated | solution.py:52
  73.4 0.2 copy.85
  73.6 0.6 copy.82
  (106 shorter events, 4.0 us)
Async XLA Ops:
  0.0 30.0 %copy-start = (bf16[4,4,128,128]{3,2,1,0:T(8,128)(2,1)S(1)}, bf16[4,4,128,128]{3,2,1,0:T(8,128)(2,1)}, u32[]{:S(2)}) copy-start(bf16[4,4,128,128]{3,2,1,0:T(8,128)(2,1)} %param.19) | copy-start | bytes 1572868
  1.6 15.0 %collective-permute-start.1 = (bf16[16,8,128]{2,0,1:T(8,128)(2,1)S(1)}, bf16[16,8,128]{2,0,1:T(8,128)(2,1)S(1)}, u32[]{:S(2)}, u32[]{:S(2)}) collective-permute-start(bf16[16,8,128]{2,0,1:T(8,128)(2,1)S(1)} %pad_maximum_fusion.3), channel_id=1, source_target_pairs={{0,1},{1,2},{2,3},{3,4},{4,5},{5,6},{6,7},{7,8},{8,9},{9,10},{10,1... | collective-permute-start | bytes 98312 | tf_op jit(solution)/shard_map/ppermute | solution.py:17
  6.8 9.8 %collective-permute-start.2 = (bf16[16,8,128]{2,0,1:T(8,128)(2,1)S(1)}, bf16[16,8,128]{2,0,1:T(8,128)(2,1)S(1)}, u32[]{:S(2)}, u32[]{:S(2)}) collective-permute-start(bf16[16,8,128]{2,0,1:T(8,128)(2,1)S(1)} %pad_maximum_fusion.3), channel_id=1, source_target_pairs={{1,0},{2,1},{3,2},{4,3},{5,4},{6,5},{7,6},{8,7},{9,8},{10,9},{11,1... | collective-permute-start | bytes 98312 | tf_op jit(solution)/shard_map/ppermute | solution.py:17
  8.7 8.0 %collective-permute-start = (bf16[12,8,128]{2,0,1:T(8,128)(2,1)S(1)}, bf16[12,8,128]{2,0,1:T(8,128)(2,1)S(1)}, u32[]{:S(2)}, u32[]{:S(2)}) collective-permute-start(bf16[12,8,128]{2,0,1:T(8,128)(2,1)S(1)} %copy.38), channel_id=1, source_target_pairs={{0,2},{1,3},{2,4},{3,5},{4,6},{5,7},{6,8},{7,9},{8,10},{9,11},{10,... | collective-permute-start | bytes 73736 | tf_op jit(solution)/shard_map/ppermute | solution.py:17
  11.6 6.8 %collective-permute-start.3 = (bf16[12,8,128]{2,0,1:T(8,128)(2,1)S(1)}, bf16[12,8,128]{2,0,1:T(8,128)(2,1)S(1)}, u32[]{:S(2)}, u32[]{:S(2)}) collective-permute-start(bf16[12,8,128]{2,0,1:T(8,128)(2,1)S(1)} %copy.38), channel_id=1, source_target_pairs={{2,0},{3,1},{4,2},{5,3},{6,4},{7,5},{8,6},{9,7},{10,8},{11,9},{12,... | collective-permute-start | bytes 73736 | tf_op jit(solution)/shard_map/ppermute | solution.py:17
  26.8 1.0 %copy-start.4 = (bf16[3,3,128,128]{3,2,1,0:T(8,128)(2,1)S(1)}, bf16[3,3,128,128]{3,2,1,0:T(8,128)(2,1)}, u32[]{:S(2)}) copy-start(bf16[3,3,128,128]{3,2,1,0:T(8,128)(2,1)} %param.17) | copy-start | bytes 884740
  26.8 1.0 %copy-start.15 = (pred[8,9]{0,1:T(8,128)(4,1)S(1)}, pred[8,9]{0,1:T(8,128)(4,1)}, u32[]{:S(2)}) copy-start(pred[8,9]{0,1:T(8,128)(4,1)} %constant.189) | copy-start | bytes 220
  27.8 1.1 %copy-start.5 = (bf16[3,3,128,128]{3,2,1,0:T(8,128)(2,1)S(1)}, bf16[3,3,128,128]{3,2,1,0:T(8,128)(2,1)}, u32[]{:S(2)}) copy-start(bf16[3,3,128,128]{3,2,1,0:T(8,128)(2,1)} %param.18) | copy-start | bytes 884740
  32.3 1.0 %copy-start.6 = (bf16[3,3,128,128]{3,2,1,0:T(8,128)(2,1)S(1)}, bf16[3,3,128,128]{3,2,1,0:T(8,128)(2,1)}, u32[]{:S(2)}) copy-start(bf16[3,3,128,128]{3,2,1,0:T(8,128)(2,1)} %param.20) | copy-start | bytes 884740
  32.3 1.0 %copy-start.14 = (pred[8,17]{0,1:T(8,128)(4,1)S(1)}, pred[8,17]{0,1:T(8,128)(4,1)}, u32[]{:S(2)}) copy-start(pred[8,17]{0,1:T(8,128)(4,1)} %constant.187) | copy-start | bytes 412
  33.3 2.6 %copy-start.12 = (bf16[3,3,4,128]{3,2,1,0:T(4,128)(2,1)S(1)}, bf16[3,3,4,128]{3,2,1,0:T(4,128)(2,1)}, u32[]{:S(2)}) copy-start(bf16[3,3,4,128]{3,2,1,0:T(4,128)(2,1)} %param.21) | copy-start | bytes 27652
  44.2 1.0 %copy-start.7 = (bf16[3,3,128,128]{3,2,1,0:T(8,128)(2,1)S(1)}, bf16[3,3,128,128]{3,2,1,0:T(8,128)(2,1)}, u32[]{:S(2)}) copy-start(bf16[3,3,128,128]{3,2,1,0:T(8,128)(2,1)} %param.23) | copy-start | bytes 884740
  45.2 1.0 %copy-start.9 = (bf16[3,3,128,128]{3,2,1,0:T(8,128)(2,1)S(1)}, bf16[3,3,128,128]{3,2,1,0:T(8,128)(2,1)}, u32[]{:S(2)}) copy-start(bf16[3,3,128,128]{3,2,1,0:T(8,128)(2,1)} %param.24) | copy-start | bytes 884740
  46.2 1.0 %copy-start.2 = (bf16[4,4,128,128]{3,2,1,0:T(8,128)(2,1)S(1)}, bf16[4,4,128,128]{3,2,1,0:T(8,128)(2,1)}, u32[]{:S(2)}) copy-start(bf16[4,4,128,128]{3,2,1,0:T(8,128)(2,1)} %param.25) | copy-start | bytes 1572868
  48.1 1.0 %copy-start.11 = (bf16[3,3,128,128]{3,2,1,0:T(8,128)(2,1)S(1)}, bf16[3,3,128,128]{3,2,1,0:T(8,128)(2,1)}, u32[]{:S(2)}) copy-start(bf16[3,3,128,128]{3,2,1,0:T(8,128)(2,1)} %param.26) | copy-start | bytes 884740
  49.0 1.1 %copy-start.13 = (bf16[3,3,4,128]{3,2,1,0:T(4,128)(2,1)S(1)}, bf16[3,3,4,128]{3,2,1,0:T(4,128)(2,1)}, u32[]{:S(2)}) copy-start(bf16[3,3,4,128]{3,2,1,0:T(4,128)(2,1)} %param.27) | copy-start | bytes 27652
  50.9 0.7 copy-start.1
  51.7 9.0 %collective-permute-start.4 = (bf16[4,8,128]{2,0,1:T(4,128)(2,1)S(1)}, bf16[4,8,128]{2,0,1:T(4,128)(2,1)S(1)}, u32[]{:S(2)}, u32[]{:S(2)}) collective-permute-start(bf16[4,8,128]{2,0,1:T(4,128)(2,1)S(1)} %multiply_convert_fusion), channel_id=1, source_target_pairs={{0,1},{1,2},{2,3},{3,4},{4,5},{5,6},{6,7},{7,8},{8,9},{9,10},{10,1... | collective-permute-start | bytes 24584 | tf_op jit(solution)/shard_map/ppermute | solution.py:17
  58.5 7.1 %collective-permute-start.5 = (bf16[4,8,128]{2,0,1:T(4,128)(2,1)S(1)}, bf16[4,8,128]{2,0,1:T(4,128)(2,1)S(1)}, u32[]{:S(2)}, u32[]{:S(2)}) collective-permute-start(bf16[4,8,128]{2,0,1:T(4,128)(2,1)S(1)} %multiply_convert_fusion), channel_id=1, source_target_pairs={{1,0},{2,1},{3,2},{4,3},{5,4},{6,5},{7,6},{8,7},{9,8},{10,9},{11,1... | collective-permute-start | bytes 24584 | tf_op jit(solution)/shard_map/ppermute | solution.py:17
  67.1 1.0 %copy-start.8 = (bf16[3,3,128,128]{3,2,1,0:T(8,128)(2,1)S(1)}, bf16[3,3,128,128]{3,2,1,0:T(8,128)(2,1)}, u32[]{:S(2)}) copy-start(bf16[3,3,128,128]{3,2,1,0:T(8,128)(2,1)} %param.23) | copy-start | bytes 884740
  68.1 1.0 %copy-start.10 = (bf16[3,3,128,128]{3,2,1,0:T(8,128)(2,1)S(1)}, bf16[3,3,128,128]{3,2,1,0:T(8,128)(2,1)}, u32[]{:S(2)}) copy-start(bf16[3,3,128,128]{3,2,1,0:T(8,128)(2,1)} %param.24) | copy-start | bytes 884740
  69.1 1.0 %copy-start.3 = (bf16[4,4,128,128]{3,2,1,0:T(8,128)(2,1)S(1)}, bf16[4,4,128,128]{3,2,1,0:T(8,128)(2,1)}, u32[]{:S(2)}) copy-start(bf16[4,4,128,128]{3,2,1,0:T(8,128)(2,1)} %param.25) | copy-start | bytes 1572868
where the time goes:
time: 75.1 us; the launch traced here: 74.2 us
  local copies, waits for them, and re-layouts  24.6 us (33%)
  starting transfers between devices  21.4 us (28%)
  matrix products  17.9 us (24%)
  waiting for transfers between devices  6.52 us (9%)
  other arithmetic  2.69 us (4%)
  between operations  1.06 us (1%)
    ppermute x6, starting transfers between devices, from_tile(): return lax.ppermute(values, 'tile', pairs)  21.4 us
    conv_general_dilated x15, matrix products, conv(): lax.conv_general_dilated(lhs, rhs, window_strides=strides, padding=paddin...  15.1 us
    unnamed x45, local copies, waits for them, and re-layouts  9.95 us
    ppermute x6, waiting for transfers between devices, from_tile(): return lax.ppermute(values, 'tile', pairs)  6.52 us
    concatenate x4, local copies, waits for them, and re-layouts, conv_in(): jnp.concatenate([padded[:, ty:ty + rows, tx:tx + cols] for ty in range(3)...  6.51 us
    conv_general_dilated x23, local copies, waits for them, and re-layouts, conv(): lax.conv_general_dilated(lhs, rhs, window_strides=strides, padding=paddin...  3.05 us
    dot_general x4, matrix products, conv_in(): jnp.einsum('krw,ko->rwo', patches, flat, preferred_element_type=jnp.float32)  2.83 us
  transfers between devices with their start and end apart: 6, of which 2 were waited for; matrix products, arithmetic and copies ran while one was open for 3% of the time, Pallas kernels for 0%

commit v1 on v0

--- a/solution.py
+++ b/solution.py
@@ -76,7 +76,10 @@
     count, _, cols = fields.shape
     lo, hi = out_lo - 1 - first, out_hi + 1 - first
     assert lo >= 0 and hi <= fields.shape[1]
-    padded = jnp.pad(fields[:, lo:hi], ((0, 0), (0, 0), (1, 1)))
+    extra = -count % 16
+    weight = jnp.pad(weight, ((0, 0), (0, 0), (0, extra), (0, 0)))
+    padded = jnp.pad(fields[:, lo:hi], ((0, extra), (0, 0), (1, 1)))
+    count += extra
     rows = out_hi - out_lo
     patches = jnp.concatenate(
         [padded[:, ty : ty + rows, tx : tx + cols] for ty in range(3) for tx in range(3)], axis=0
@@ -108,11 +111,22 @@
     joined = row_mask(joined, join_lo, base, grid_rows).astype(jnp.bfloat16)
     refined = conv(joined[None], w_fine, ("NHWC", "HWIO", "NHWC"))[0]
     refined = row_mask(silu(refined), join_lo + 1, base, grid_rows).astype(jnp.bfloat16)
-    out_count = w_out.shape[2]
-    lanes = w_out.shape[3]
-    w_wide = jnp.pad(w_out, ((0, 0), (0, 0), (0, lanes - out_count), (0, 0)))
-    result = conv(refined[None], w_wide, ("NHWC", "HWOI", "NHWC"))[0]
-    return jnp.transpose(result[..., :out_count], (2, 0, 1))
+    return conv_out(refined, w_out)
+
+
+def conv_out(refined, weight):
+    count, cols = refined.shape[0] - 2, refined.shape[1]
+    outs = weight.shape[2]
+    flat = weight.reshape(9 * outs, weight.shape[3])
+    planes = jnp.einsum("tc,rwc->trw", flat, refined, preferred_element_type=jnp.float32)
+    planes = jnp.pad(planes, ((0, 0), (0, 0), (1, 1)))
+    total = None
+    for ty in range(3):
+        for tx in range(3):
+            tap = (ty * 3 + tx) * outs
+            term = planes[tap : tap + outs, ty : ty + count, tx : tx + cols]
+            total = term if total is None else total + term
+    return total
 
 
 def shards(

time: 75.1 us -> 68.8 us (0.916)
  the two profiles are of different devices: /device:TPU:415 before, /device:TPU:351 now
where the time goes in v1:
time: 68.8 us; the launch traced here: 68 us
  starting transfers between devices  23 us (33%)
  local copies, waits for them, and re-layouts  17.5 us (25%)
  matrix products  17 us (25%)
  waiting for transfers between devices  4.93 us (7%)
  other arithmetic  4.54 us (7%)
  between operations  1.13 us (2%)
    ppermute x6, starting transfers between devices, from_tile(): return lax.ppermute(values, 'tile', pairs)  23 us
    conv_general_dilated x12, matrix products, conv(): lax.conv_general_dilated(lhs, rhs, window_strides=strides, padding=paddin...  12 us
    unnamed x78, local copies, waits for them, and re-layouts  9.72 us
    ppermute x6, waiting for transfers between devices, from_tile(): return lax.ppermute(values, 'tile', pairs)  4.93 us
    dot_general x4, matrix products, conv_in(): jnp.einsum('krw,ko->rwo', patches, flat, preferred_element_type=jnp.float32)  3.44 us
    conv_general_dilated x17, local copies, waits for them, and re-layouts, conv(): lax.conv_general_dilated(lhs, rhs, window_strides=strides, padding=paddin...  2.34 us
    dot_general x3, matrix products, conv_out(): jnp.einsum('tc,rwc->trw', flat, refined, preferred_element_type=jnp.float32)  1.5 us
    reshape x2, local copies, waits for them, and re-layouts, conv_out(): flat = weight.reshape(9 * outs, weight.shape[3])  1.43 us
  transfers between devices with their start and end apart: 6, of which 1 were waited for; matrix products, arithmetic and copies ran while one was open for 6% of the time, Pallas kernels for 0%

profile of v1, /device:TPU:351, one launch (start us, length us, event | category | flops | bytes accessed | tf_op | source)
XLA Modules:
  0.0 68.0 jit_solution(3515503601809355776)
XLA Ops:
  0.0 0.8 %copy.35 = bf16[12,8,128]{2,0,1:T(8,128)(2,1)S(1)} copy(bf16[12,8,128]{2,1,0:T(8,128)(2,1)} %param.14) | data formatting | bytes 49152 | tf_op args[0]
  0.8 0.7 %fusion.250 = bf16[4,8,128]{2,0,1:T(4,128)(2,1)S(1)} fusion(f32[1,4,8,128]{3,2,1,0:T(8,128)} %param.15), kind=kLoop, calls=%fused_computation.311 | loop fusion | flops 8192 | bytes 24576 | tf_op jit(solution)/shard_map/convert_element_type | solution.py:173
  1.6 5.2 %collective-permute-start.1 = (bf16[16,8,128]{2,0,1:T(8,128)(2,1)S(1)}, bf16[16,8,128]{2,0,1:T(8,128)(2,1)S(1)}, u32[]{:S(2)}, u32[]{:S(2)}) collective-permute-start(bf16[16,8,128]{2,0,1:T(8,128)(2,1)S(1)} %pad_maximum_fusion.2), channel_id=1, source_target_pairs={{0,1},{1,2},{2,3},{3,4},{4,5},{5,6},{6,7},{7,8},{8,9},{9,10},{10,1... | collective-permute-start | bytes 98312 | tf_op jit(solution)/shard_map/ppermute | solution.py:17
  6.8 1.9 %collective-permute-start.2 = (bf16[16,8,128]{2,0,1:T(8,128)(2,1)S(1)}, bf16[16,8,128]{2,0,1:T(8,128)(2,1)S(1)}, u32[]{:S(2)}, u32[]{:S(2)}) collective-permute-start(bf16[16,8,128]{2,0,1:T(8,128)(2,1)S(1)} %pad_maximum_fusion.2), channel_id=1, source_target_pairs={{1,0},{2,1},{3,2},{4,3},{5,4},{6,5},{7,6},{8,7},{9,8},{10,9},{11,1... | collective-permute-start | bytes 98312 | tf_op jit(solution)/shard_map/ppermute | solution.py:17
  8.7 2.8 %collective-permute-start = (bf16[12,8,128]{2,0,1:T(8,128)(2,1)S(1)}, bf16[12,8,128]{2,0,1:T(8,128)(2,1)S(1)}, u32[]{:S(2)}, u32[]{:S(2)}) collective-permute-start(bf16[12,8,128]{2,0,1:T(8,128)(2,1)S(1)} %copy.35), channel_id=1, source_target_pairs={{0,2},{1,3},{2,4},{3,5},{4,6},{5,7},{6,8},{7,9},{8,10},{9,11},{10,... | collective-permute-start | bytes 73736 | tf_op jit(solution)/shard_map/ppermute | solution.py:17
  11.6 2.5 %collective-permute-start.3 = (bf16[12,8,128]{2,0,1:T(8,128)(2,1)S(1)}, bf16[12,8,128]{2,0,1:T(8,128)(2,1)S(1)}, u32[]{:S(2)}, u32[]{:S(2)}) collective-permute-start(bf16[12,8,128]{2,0,1:T(8,128)(2,1)S(1)} %copy.35), channel_id=1, source_target_pairs={{2,0},{3,1},{4,2},{5,3},{6,4},{7,5},{8,6},{9,7},{10,8},{11,9},{12,... | collective-permute-start | bytes 73736 | tf_op jit(solution)/shard_map/ppermute | solution.py:17
  14.2 0.5 compare_and_fusion.1
  14.7 1.0 %slice_select_fusion = (bf16[3,3,16,128]{3,2,1,0:T(8,128)(2,1)S(1)}, bf16[3,3,16,128]{3,2,1,0:T(8,128)(2,1)S(1)}) fusion(bf16[3,3,20,128]{3,2,1,0:T(8,128)(2,1)} %param.22, pred[16]{0:T(512)(128)(4,1)} %constant.53.clone.1), kind=kLoop, calls=%fused_computation.287 | loop fusion | flops 18432 | bytes 147472 | tf_op jit(solution)/shard_map/jit(_pad)/pad | solution.py:80
  15.7 0.6 compare_and_fusion.4
  16.3 0.7 %reshape.273 = bf16[36,128,1]{1,0,2:T(8,128)(2,1)S(1)} reshape(bf16[3,3,4,128]{3,2,1,0:T(4,128)(2,1)} %param.21) | data formatting | bytes 18432 | tf_op jit(solution)/shard_map/reshape | solution.py:120
  17.0 0.7 %reshape.276 = bf16[36,128,1]{1,0,2:T(8,128)(2,1)S(1)} reshape(bf16[3,3,4,128]{3,2,1,0:T(4,128)(2,1)} %param.27) | data formatting | bytes 18432 | tf_op jit(solution)/shard_map/reshape | solution.py:120
  17.7 0.8 %pad.36 = bf16[3,3,16,128]{3,2,1,0:T(8,128)(2,1)S(1)} pad(bf16[3,3,12,128]{3,2,1,0:T(8,128)(2,1)} %param.16, bf16[]{:T(256)} %constant.43.clone.1), padding=0_0x0_0x0_4x0_0 | pad | bytes 64514 | tf_op jit(solution)/shard_map/jit(_pad)/pad | solution.py:80
  18.6 0.2 fusion.135
  19.7 1.3 %select_convert_fusion = bf16[37,128,128]{2,1,0:T(8,128)(2,1)S(1)} fusion(bf16[144,37,128]{2,0,1:T(8,128)(2,1)S(1)} %slice_dynamic-update-slice_fusion, bf16[144,128,1]{1,0,2:T(8,128)(2,1)S(1)} %bitcast.206, pred[37]{0:T(512)(128)(4,1)S(1)} %compare_and_fusion.7), kind=kOutput, calls=%fused_computation.2 | convolution fusion | flops 178225152 | bytes 2613285 | tf_op jit(solution)/shard_map/krw,ko->rwo/dot_general | solution.py:88
  21.0 0.8 %copy.79 = bf16[37,1,128,128]{3,0,2,1:T(8,128)(2,1)S(1)} copy(bf16[37,1,128,128]{3,2,0,1:T(8,128)(2,1)S(1)} %bitcast.191) | data formatting | bytes 2424832
  21.8 0.2 pad.44.clone
  22.1 0.4 copy.41
  22.5 0.5 copy-done.3
  23.1 1.0 %fusion.48 = bf16[18,1,8,9,128]{4,2,3,0,1:T(8,128)(2,1)S(1)} fusion(bf16[3,3,128,128]{3,2,1,0:T(8,128)(2,1)S(1)} %copy-done.3, bf16[37,1,7,2,128]{4,2,3,0,1:T(8,128)(2,1)S(1)} %slice.354, bf16[37,1,8,18,128]{4,2,3,0,1:T(8,128)(2,1)S(1)} %copy.41, pred[18]{0:T(512)(128)(4,1)S(1)} %compare_and_fusion.5, pred[8,9]{0,1:T(8,128)(4,1)S(1)} %copy-done.20), kind=kOutput, calls=%fused_computation.84 | convolution fusion | flops 388079616 | bytes 2123354 | tf_op jit(solution)/shard_map/conv_general_dilated | solution.py:52
  24.1 0.9 %fusion.83 = bf16[16,8,9,128]{3,1,2,0:T(8,128)(2,1)S(1)} fusion(bf16[3,3,128,128]{3,2,1,0:T(8,128)(2,1)S(1)} %copy-done.4, bf16[18,1,7,1,128]{4,2,3,0,1:T(8,128)(2,1)S(1)} %get-tuple-element.10, bf16[18,1,7,1,128]{4,2,3,0,1:T(8,128)(2,1)S(1)} %get-tuple-element.9, bf16[18,1,8,9,128]{4,2,3,0,1:T(8,128)(2,1)S(1)} %fusion.48, ...), kind=kOutput, calls=%fused_computation.120 | convolution fusion | flops 342798336 | bytes 986200 | tf_op jit(solution)/shard_map/conv_general_dilated | solution.py:52
  25.3 1.1 %fusion.120 = f32[28,8,16,128]{3,1,2,0:T(8,128)S(1)} fusion(bf16[4,4,128,128]{3,2,1,0:T(8,128)(2,1)S(1)} %copy-done, bf16[16,1,7,1,128]{4,2,3,0,1:T(8,128)(2,1)S(1)} %get-tuple-element.12, bf16[16,1,7,1,128]{4,2,3,0,1:T(8,128)(2,1)S(1)} %get-tuple-element.11, bf16[16,1,8,8,128]{4,2,3,0,1:T(8,128)(2,1)S(1)} %copy.44), kind=kOutput, calls=%fused_computation.145 | convolution fusion | flops 471400448 | bytes 2678784 | tf_op jit(solution)/shard_map/conv_general_dilated | solution.py:52
  26.4 0.3 copy.47
  26.7 0.3 fusion.3
  27.0 0.6 copy.80
  27.6 0.2 pad.50.clone
  27.9 0.4 copy.50
  28.3 0.5 copy-done.5
  28.8 2.4 %select_convert_fusion.1 = bf16[26,8,17,128]{3,1,2,0:T(8,128)(2,1)S(1)} fusion(bf16[3,3,128,128]{3,2,1,0:T(8,128)(2,1)S(1)} %copy-done.5, bf16[28,1,7,2,128]{4,2,3,0,1:T(8,128)(2,1)S(1)} %slice.360, bf16[28,1,8,17,128]{4,2,3,0,1:T(8,128)(2,1)S(1)} %copy.50, pred[26]{0:T(512)(128)(4,1)S(1)} %compare_and_fusion.9, pred[8,17]{0,1:T(8,128)(4,1)S(1)} %copy-done.11), kind=kOutput, calls=%fused_computation.14 | convolution fusion | flops 1049245696 | bytes 2275490 | tf_op jit(solution)/shard_map/conv_general_dilated | solution.py:52
  31.3 0.2 copy.51
  31.5 0.8 %convolution_bitcast_fusion = f32[36,26,128]{2,0,1:T(8,128)S(1)} fusion(bf16[36,128,1]{1,0,2:T(8,128)(2,1)S(1)} %reshape.273, bf16[26,1,128,128]{3,0,2,1:T(8,128)(2,1)S(1)} %slice.361), kind=kOutput, calls=%fused_computation.31 | convolution fusion | flops 30670848 | bytes 1340416 | tf_op jit(solution)/shard_map/tc,rwc->trw/dot_general | solution.py:121
  32.4 0.2 fusion.295
  34.4 0.6 fusion.303
  35.0 0.8 %select_convert_fusion.3 = bf16[21,128,128]{2,1,0:T(8,128)(2,1)S(1)} fusion(f32[21,128,128]{2,1,0:T(8,128)S(1)} %fusion.303, bf16[144,21,128]{2,0,1:T(8,128)(2,1)S(1)} %slice_dynamic-update-slice_fusion.18, bf16[144,128,1]{1,0,2:T(8,128)(2,1)S(1)} %bitcast.207, pred[21]{0:T(512)(128)(4,1)S(1)} %compare_and_fusion.2), kind=kOutput, calls=%fused_computation.27 | convolution fusion | flops 101498880 | bytes 2875413 | tf_op jit(solution)/shard_map/krw,ko->rwo/dot_general | solution.py:88
  35.7 0.5 copy.81
  36.2 0.2 pad.52.clone
  36.4 0.2 copy.55
  36.6 0.5 copy-done.6
  37.2 0.6 fusion.115
  37.8 0.3 copy-done.8
  38.1 0.5 fusion.147
  38.8 0.4 copy-done.2
  39.2 0.6 fusion.188
  39.7 0.1 copy.61
  40.2 0.2 reshape.189
  40.4 0.3 copy-done.12
  40.7 2.0 %select_convert_fusion.5 = bf16[10,8,17,128]{3,1,2,0:T(8,128)(2,1)S(1)} fusion(bf16[3,3,128,128]{3,2,1,0:T(8,128)(2,1)} %param.26, bf16[12,1,7,2,128]{4,2,3,0,1:T(8,128)(2,1)S(1)} %slice.388, bf16[12,1,8,17,128]{4,2,3,0,1:T(8,128)(2,1)S(1)} %copy.63, pred[10]{0:T(512)(128)(4,1)S(1)} %copy-done.12, pred[8,17]{0,1:T(8,128)(4,1)S(1)} %copy-done.11), kind=kOutput, calls=%fused_computation.81 | convolution fusion | flops 403699712 | bytes 1104018 | tf_op jit(solution)/shard_map/conv_general_dilated | solution.py:52
  43.0 0.3 convolution_bitcast_fusion.2
  43.6 8.4 %collective-permute-start.4 = (bf16[4,8,128]{2,0,1:T(4,128)(2,1)S(1)}, bf16[4,8,128]{2,0,1:T(4,128)(2,1)S(1)}, u32[]{:S(2)}, u32[]{:S(2)}) collective-permute-start(bf16[4,8,128]{2,0,1:T(4,128)(2,1)S(1)} %get-tuple-element.5), channel_id=1, source_target_pairs={{0,1},{1,2},{2,3},{3,4},{4,5},{5,6},{6,7},{7,8},{8,9},{9,10},{10,1... | collective-permute-start | bytes 24584 | tf_op jit(solution)/shard_map/ppermute | solution.py:17
  52.0 2.1 %collective-permute-start.5 = (bf16[4,8,128]{2,0,1:T(4,128)(2,1)S(1)}, bf16[4,8,128]{2,0,1:T(4,128)(2,1)S(1)}, u32[]{:S(2)}, u32[]{:S(2)}) collective-permute-start(bf16[4,8,128]{2,0,1:T(4,128)(2,1)S(1)} %get-tuple-element.5), channel_id=1, source_target_pairs={{1,0},{2,1},{3,2},{4,3},{5,4},{6,5},{7,6},{8,7},{9,8},{10,9},{11,1... | collective-permute-start | bytes 24584 | tf_op jit(solution)/shard_map/ppermute | solution.py:17
  54.1 4.9 %collective-permute-done.5 = bf16[4,8,128]{2,0,1:T(4,128)(2,1)S(1)} collective-permute-done((bf16[4,8,128]{2,0,1:T(4,128)(2,1)S(1)}, bf16[4,8,128]{2,0,1:T(4,128)(2,1)S(1)}, u32[]{:S(2)}, u32[]{:S(2)}) %collective-permute-start.5) | collective-permute-done | bytes 8224 | tf_op jit(solution)/shard_map/ppermute | solution.py:17
  60.0 0.8 %select_convert_fusion.2 = bf16[21,128,128]{2,1,0:T(8,128)(2,1)S(1)} fusion(f32[21,128,128]{2,1,0:T(8,128)S(1)} %fusion.303, bf16[144,21,128]{2,0,1:T(8,128)(2,1)S(1)} %slice_dynamic-update-slice_fusion.9, bf16[144,128,1]{1,0,2:T(8,128)(2,1)S(1)} %bitcast.208, pred[21]{0:T(512)(128)(4,1)S(1)} %copy-done.19), kind=kOutput, calls=%fused_computation.26 | convolution fusion | flops 101498880 | bytes 2875413 | tf_op jit(solution)/shard_map/krw,ko->rwo/dot_general | solution.py:88
  60.7 0.5 copy.82
  61.2 0.2 pad.60.clone
  61.4 0.2 copy.67
  61.7 0.5 copy-done.7
  62.2 0.7 fusion.107
  62.9 0.3 copy-done.9
  63.1 0.5 fusion.157
  63.8 0.6 fusion.193
  64.8 0.2 reshape.213
  65.1 0.6 copy-done.10
  65.6 1.0 %select_convert_fusion.4 = bf16[10,8,17,128]{3,1,2,0:T(8,128)(2,1)S(1)} fusion(bf16[3,3,128,128]{3,2,1,0:T(8,128)(2,1)S(1)} %copy-done.10, bf16[12,1,7,2,128]{4,2,3,0,1:T(8,128)(2,1)S(1)} %slice.409, bf16[12,1,8,17,128]{4,2,3,0,1:T(8,128)(2,1)S(1)} %copy.75, pred[10]{0:T(512)(128)(4,1)S(1)} %copy-done.13, pred[8,17]{0,1:T(8,128)(4,1)S(1)} %copy-done.11), kind=kOutput, calls=%fused_computation.80 | convolution fusion | flops 403699712 | bytes 1104018 | tf_op jit(solution)/shard_map/conv_general_dilated | solution.py:52
  66.9 0.3 convolution_bitcast_fusion.1
  67.4 0.6 copy.77
  (129 shorter events, 5.8 us)
Async XLA Ops:
  0.0 25.3 %copy-start = (bf16[4,4,128,128]{3,2,1,0:T(8,128)(2,1)S(1)}, bf16[4,4,128,128]{3,2,1,0:T(8,128)(2,1)}, u32[]{:S(2)}) copy-start(bf16[4,4,128,128]{3,2,1,0:T(8,128)(2,1)} %param.19) | copy-start | bytes 1572868
  1.6 16.9 %collective-permute-start.1 = (bf16[16,8,128]{2,0,1:T(8,128)(2,1)S(1)}, bf16[16,8,128]{2,0,1:T(8,128)(2,1)S(1)}, u32[]{:S(2)}, u32[]{:S(2)}) collective-permute-start(bf16[16,8,128]{2,0,1:T(8,128)(2,1)S(1)} %pad_maximum_fusion.2), channel_id=1, source_target_pairs={{0,1},{1,2},{2,3},{3,4},{4,5},{5,6},{6,7},{7,8},{8,9},{9,10},{10,1... | collective-permute-start | bytes 98312 | tf_op jit(solution)/shard_map/ppermute | solution.py:17
  6.8 11.7 %collective-permute-start.2 = (bf16[16,8,128]{2,0,1:T(8,128)(2,1)S(1)}, bf16[16,8,128]{2,0,1:T(8,128)(2,1)S(1)}, u32[]{:S(2)}, u32[]{:S(2)}) collective-permute-start(bf16[16,8,128]{2,0,1:T(8,128)(2,1)S(1)} %pad_maximum_fusion.2), channel_id=1, source_target_pairs={{1,0},{2,1},{3,2},{4,3},{5,4},{6,5},{7,6},{8,7},{9,8},{10,9},{11,1... | collective-permute-start | bytes 98312 | tf_op jit(solution)/shard_map/ppermute | solution.py:17
  8.7 9.9 %collective-permute-start = (bf16[12,8,128]{2,0,1:T(8,128)(2,1)S(1)}, bf16[12,8,128]{2,0,1:T(8,128)(2,1)S(1)}, u32[]{:S(2)}, u32[]{:S(2)}) collective-permute-start(bf16[12,8,128]{2,0,1:T(8,128)(2,1)S(1)} %copy.35), channel_id=1, source_target_pairs={{0,2},{1,3},{2,4},{3,5},{4,6},{5,7},{6,8},{7,9},{8,10},{9,11},{10,... | collective-permute-start | bytes 73736 | tf_op jit(solution)/shard_map/ppermute | solution.py:17
  11.6 7.0 %collective-permute-start.3 = (bf16[12,8,128]{2,0,1:T(8,128)(2,1)S(1)}, bf16[12,8,128]{2,0,1:T(8,128)(2,1)S(1)}, u32[]{:S(2)}, u32[]{:S(2)}) collective-permute-start(bf16[12,8,128]{2,0,1:T(8,128)(2,1)S(1)} %copy.35), channel_id=1, source_target_pairs={{2,0},{3,1},{4,2},{5,3},{6,4},{7,5},{8,6},{9,7},{10,8},{11,9},{12,... | collective-permute-start | bytes 73736 | tf_op jit(solution)/shard_map/ppermute | solution.py:17
  14.2 20.8 %copy-start.18 = (pred[21]{0:T(512)(128)(4,1)}, pred[21]{0:T(512)(128)(4,1)S(1)}, u32[]{:S(2)}) copy-start(pred[21]{0:T(512)(128)(4,1)S(1)} %compare_and_fusion.2) | copy-start | bytes 67
  14.2 22.4 %copy-start.16 = (pred[10]{0:T(512)(128)(4,1)}, pred[10]{0:T(512)(128)(4,1)S(1)}, u32[]{:S(2)}) copy-start(pred[10]{0:T(512)(128)(4,1)S(1)} %compare_and_fusion) | copy-start | bytes 34
  22.1 1.0 %copy-start.3 = (bf16[3,3,128,128]{3,2,1,0:T(8,128)(2,1)S(1)}, bf16[3,3,128,128]{3,2,1,0:T(8,128)(2,1)}, u32[]{:S(2)}) copy-start(bf16[3,3,128,128]{3,2,1,0:T(8,128)(2,1)} %param.17) | copy-start | bytes 884740
  22.1 1.0 %copy-start.20 = (pred[8,9]{0,1:T(8,128)(4,1)S(1)}, pred[8,9]{0,1:T(8,128)(4,1)}, u32[]{:S(2)}) copy-start(pred[8,9]{0,1:T(8,128)(4,1)} %constant.186) | copy-start | bytes 220
  23.1 1.1 %copy-start.4 = (bf16[3,3,128,128]{3,2,1,0:T(8,128)(2,1)S(1)}, bf16[3,3,128,128]{3,2,1,0:T(8,128)(2,1)}, u32[]{:S(2)}) copy-start(bf16[3,3,128,128]{3,2,1,0:T(8,128)(2,1)} %param.18) | copy-start | bytes 884740
  27.8 1.0 %copy-start.5 = (bf16[3,3,128,128]{3,2,1,0:T(8,128)(2,1)S(1)}, bf16[3,3,128,128]{3,2,1,0:T(8,128)(2,1)}, u32[]{:S(2)}) copy-start(bf16[3,3,128,128]{3,2,1,0:T(8,128)(2,1)} %param.20) | copy-start | bytes 884740
  27.9 1.0 %copy-start.11 = (pred[8,17]{0,1:T(8,128)(4,1)S(1)}, pred[8,17]{0,1:T(8,128)(4,1)}, u32[]{:S(2)}) copy-start(pred[8,17]{0,1:T(8,128)(4,1)} %constant.185) | copy-start | bytes 412
  36.2 1.0 %copy-start.6 = (bf16[3,3,128,128]{3,2,1,0:T(8,128)(2,1)S(1)}, bf16[3,3,128,128]{3,2,1,0:T(8,128)(2,1)}, u32[]{:S(2)}) copy-start(bf16[3,3,128,128]{3,2,1,0:T(8,128)(2,1)} %param.23) | copy-start | bytes 884740
  37.2 1.0 %copy-start.8 = (bf16[3,3,128,128]{3,2,1,0:T(8,128)(2,1)S(1)}, bf16[3,3,128,128]{3,2,1,0:T(8,128)(2,1)}, u32[]{:S(2)}) copy-start(bf16[3,3,128,128]{3,2,1,0:T(8,128)(2,1)} %param.24) | copy-start | bytes 884740
  37.2 1.0 %copy-start.14 = (pred[8]{0:T(512)(128)(4,1)S(1)}, pred[8]{0:T(512)(128)(4,1)}, u32[]{:S(2)}) copy-start(pred[8]{0:T(512)(128)(4,1)} %compare_and_fusion.1) | copy-start | bytes 28
  38.1 1.0 %copy-start.2 = (bf16[4,4,128,128]{3,2,1,0:T(8,128)(2,1)S(1)}, bf16[4,4,128,128]{3,2,1,0:T(8,128)(2,1)}, u32[]{:S(2)}) copy-start(bf16[4,4,128,128]{3,2,1,0:T(8,128)(2,1)} %param.25) | copy-start | bytes 1572868
  40.0 0.7 copy-start.12
  42.7 0.7 %copy-start.1 = (f32[1,4,8,128]{3,2,1,0:T(8,128)S(1)}, f32[1,4,8,128]{3,2,1,0:T(8,128)}, u32[]{:S(2)}) copy-start(f32[1,4,8,128]{3,2,1,0:T(8,128)} %param.15) | copy-start | bytes 49156
  43.0 17.0 %copy-start.19 = (pred[21]{0:T(512)(128)(4,1)S(1)}, pred[21]{0:T(512)(128)(4,1)}, u32[]{:S(2)}) copy-start(pred[21]{0:T(512)(128)(4,1)} %copy-done.18) | copy-start | bytes 67
  43.6 10.6 %collective-permute-start.4 = (bf16[4,8,128]{2,0,1:T(4,128)(2,1)S(1)}, bf16[4,8,128]{2,0,1:T(4,128)(2,1)S(1)}, u32[]{:S(2)}, u32[]{:S(2)}) collective-permute-start(bf16[4,8,128]{2,0,1:T(4,128)(2,1)S(1)} %get-tuple-element.5), channel_id=1, source_target_pairs={{0,1},{1,2},{2,3},{3,4},{4,5},{5,6},{6,7},{7,8},{8,9},{9,10},{10,1... | collective-permute-start | bytes 24584 | tf_op jit(solution)/shard_map/ppermute | solution.py:17
  52.0 7.1 %collective-permute-start.5 = (bf16[4,8,128]{2,0,1:T(4,128)(2,1)S(1)}, bf16[4,8,128]{2,0,1:T(4,128)(2,1)S(1)}, u32[]{:S(2)}, u32[]{:S(2)}) collective-permute-start(bf16[4,8,128]{2,0,1:T(4,128)(2,1)S(1)} %get-tuple-element.5), channel_id=1, source_target_pairs={{1,0},{2,1},{3,2},{4,3},{5,4},{6,5},{7,6},{8,7},{9,8},{10,9},{11,1... | collective-permute-start | bytes 24584 | tf_op jit(solution)/shard_map/ppermute | solution.py:17
  61.2 1.0 %copy-start.7 = (bf16[3,3,128,128]{3,2,1,0:T(8,128)(2,1)S(1)}, bf16[3,3,128,128]{3,2,1,0:T(8,128)(2,1)}, u32[]{:S(2)}) copy-start(bf16[3,3,128,128]{3,2,1,0:T(8,128)(2,1)} %param.23) | copy-start | bytes 884740
  61.2 1.0 %copy-start.17 = (pred[10]{0:T(512)(128)(4,1)S(1)}, pred[10]{0:T(512)(128)(4,1)}, u32[]{:S(2)}) copy-start(pred[10]{0:T(512)(128)(4,1)} %copy-done.16) | copy-start | bytes 34
  61.2 0.9 %copy-start.21 = (pred[8,9]{0,1:T(8,128)(4,1)S(1)}, pred[8,9]{0,1:T(8,128)(4,1)}, u32[]{:S(2)}) copy-start(pred[8,9]{0,1:T(8,128)(4,1)} %constant.186) | copy-start | bytes 220
  62.2 1.0 %copy-start.9 = (bf16[3,3,128,128]{3,2,1,0:T(8,128)(2,1)S(1)}, bf16[3,3,128,128]{3,2,1,0:T(8,128)(2,1)}, u32[]{:S(2)}) copy-start(bf16[3,3,128,128]{3,2,1,0:T(8,128)(2,1)} %param.24) | copy-start | bytes 884740
  62.2 1.0 %copy-start.15 = (pred[8]{0:T(512)(128)(4,1)S(1)}, pred[8]{0:T(512)(128)(4,1)}, u32[]{:S(2)}) copy-start(pred[8]{0:T(512)(128)(4,1)} %compare_and_fusion.1) | copy-start | bytes 28
  64.7 1.0 %copy-start.10 = (bf16[3,3,128,128]{3,2,1,0:T(8,128)(2,1)S(1)}, bf16[3,3,128,128]{3,2,1,0:T(8,128)(2,1)}, u32[]{:S(2)}) copy-start(bf16[3,3,128,128]{3,2,1,0:T(8,128)(2,1)} %param.26) | copy-start | bytes 884740
  64.7 1.0 %copy-start.13 = (pred[10]{0:T(512)(128)(4,1)S(1)}, pred[10]{0:T(512)(128)(4,1)}, u32[]{:S(2)}) copy-start(pred[10]{0:T(512)(128)(4,1)} %compare_and_fusion.4) | copy-start | bytes 34

commit v2 on v1

--- a/solution.py
+++ b/solution.py
@@ -102,7 +102,7 @@
     middle = row_mask(silu(middle), mid_lo, base // 2, grid_rows // 2).astype(jnp.bfloat16)
     upward = conv(
         middle[None],
-        w_up[::-1, ::-1],
+        w_up,
         ("NHWC", "HWIO", "NHWC"),
         padding=((0, 0), (2, 2)),
         dilation=(2, 2),
@@ -114,10 +114,9 @@
     return conv_out(refined, w_out)
 
 
-def conv_out(refined, weight):
+def conv_out(refined, flat):
     count, cols = refined.shape[0] - 2, refined.shape[1]
-    outs = weight.shape[2]
-    flat = weight.reshape(9 * outs, weight.shape[3])
+    outs = flat.shape[0] // 9
     planes = jnp.einsum("tc,rwc->trw", flat, refined, preferred_element_type=jnp.float32)
     planes = jnp.pad(planes, ((0, 0), (0, 0), (1, 1)))
     total = None
@@ -148,8 +147,22 @@
     rows = conditioning.shape[1]
     grid_rows = rows * lax.axis_size("tile")
     base = lax.axis_index("tile") * rows
-    reg_weights = (reg_in, reg_down, reg_low, reg_up, reg_fine, reg_out)
-    dif_weights = (dif_in, dif_down, dif_low, dif_up, dif_fine, dif_out)
+    keep = base >= 0
+
+    def staged(weights):
+        w_in, w_down, w_low, w_up, w_fine, w_out = weights
+        inner = (
+            w_down,
+            w_low,
+            w_up[::-1, ::-1],
+            w_fine,
+            w_out.reshape(9 * w_out.shape[2], w_out.shape[3]),
+        )
+        inner = tuple(jnp.where(keep, w, jnp.zeros_like(w)) for w in inner)
+        return (w_in,) + lax.optimization_barrier(inner)
+
+    reg_weights = staged((reg_in, reg_down, reg_low, reg_up, reg_fine, reg_out))
+    dif_weights = staged((dif_in, dif_down, dif_low, dif_up, dif_fine, dif_out))
     cond_count = conditioning.shape[0]
     noise_count = member_noise.shape[1]
 

time: 68.8 us -> 68.5 us (level)
  the two profiles are of different devices: /device:TPU:351 before, /device:TPU:223 now
where the time goes in v2:
time: 68.5 us; the launch traced here: 67.9 us
  starting transfers between devices  23 us (34%)
  matrix products  16.4 us (24%)
  local copies, waits for them, and re-layouts  15.3 us (22%)
  other arithmetic  7.04 us (10%)
  waiting for transfers between devices  4.93 us (7%)
  between operations  1.19 us (2%)
    ppermute x6, starting transfers between devices, from_tile(): return lax.ppermute(values, 'tile', pairs)  23 us
    conv_general_dilated x12, matrix products, conv(): lax.conv_general_dilated(lhs, rhs, window_strides=strides, padding=paddin...  10.9 us
    unnamed x84, local copies, waits for them, and re-layouts  9.3 us
    ppermute x6, waiting for transfers between devices, from_tile(): return lax.ppermute(values, 'tile', pairs)  4.93 us
    conv_general_dilated x23, local copies, waits for them, and re-layouts, conv(): lax.conv_general_dilated(lhs, rhs, window_strides=strides, padding=paddin...  3.51 us
    dot_general x4, matrix products, conv_in(): jnp.einsum('krw,ko->rwo', patches, flat, preferred_element_type=jnp.float32)  3.43 us
    and x11, other arithmetic, row_mask(): keep = (index >= 0) & (index < limit)  2.91 us
    dot_general x3, matrix products, conv_out(): jnp.einsum('tc,rwc->trw', flat, refined, preferred_element_type=jnp.float32)  2.1 us
  transfers between devices with their start and end apart: 6, of which 1 were waited for; matrix products, arithmetic and copies ran while one was open for 7% of the time, Pallas kernels for 0%

profile of v2, /device:TPU:223, one launch (start us, length us, event | category | flops | bytes accessed | tf_op | source)
XLA Modules:
  0.0 67.9 jit_solution(17718310017956336959)
XLA Ops:
  0.0 0.8 %copy.78 = bf16[12,8,128]{2,0,1:T(8,128)(2,1)S(1)} copy(bf16[12,8,128]{2,1,0:T(8,128)(2,1)} %param.14) | data formatting | bytes 49152 | tf_op args[0]
  0.8 0.7 %fusion.253 = bf16[4,8,128]{2,0,1:T(4,128)(2,1)S(1)} fusion(f32[1,4,8,128]{3,2,1,0:T(8,128)} %param.15), kind=kLoop, calls=%fused_computation.320 | loop fusion | flops 8192 | bytes 24576 | tf_op jit(solution)/shard_map/convert_element_type | solution.py:186
  1.6 5.2 %collective-permute-start.1 = (bf16[16,8,128]{2,0,1:T(8,128)(2,1)S(1)}, bf16[16,8,128]{2,0,1:T(8,128)(2,1)S(1)}, u32[]{:S(2)}, u32[]{:S(2)}) collective-permute-start(bf16[16,8,128]{2,0,1:T(8,128)(2,1)S(1)} %pad_maximum_fusion.2), channel_id=1, source_target_pairs={{0,1},{1,2},{2,3},{3,4},{4,5},{5,6},{6,7},{7,8},{8,9},{9,10},{10,1... | collective-permute-start | bytes 98312 | tf_op jit(solution)/shard_map/ppermute | solution.py:17
  6.8 1.9 %collective-permute-start.2 = (bf16[16,8,128]{2,0,1:T(8,128)(2,1)S(1)}, bf16[16,8,128]{2,0,1:T(8,128)(2,1)S(1)}, u32[]{:S(2)}, u32[]{:S(2)}) collective-permute-start(bf16[16,8,128]{2,0,1:T(8,128)(2,1)S(1)} %pad_maximum_fusion.2), channel_id=1, source_target_pairs={{1,0},{2,1},{3,2},{4,3},{5,4},{6,5},{7,6},{8,7},{9,8},{10,9},{11,1... | collective-permute-start | bytes 98312 | tf_op jit(solution)/shard_map/ppermute | solution.py:17
  8.7 2.8 %collective-permute-start = (bf16[12,8,128]{2,0,1:T(8,128)(2,1)S(1)}, bf16[12,8,128]{2,0,1:T(8,128)(2,1)S(1)}, u32[]{:S(2)}, u32[]{:S(2)}) collective-permute-start(bf16[12,8,128]{2,0,1:T(8,128)(2,1)S(1)} %copy.78), channel_id=1, source_target_pairs={{0,2},{1,3},{2,4},{3,5},{4,6},{5,7},{6,8},{7,9},{8,10},{9,11},{10,... | collective-permute-start | bytes 73736 | tf_op jit(solution)/shard_map/ppermute | solution.py:17
  11.6 2.5 %collective-permute-start.3 = (bf16[12,8,128]{2,0,1:T(8,128)(2,1)S(1)}, bf16[12,8,128]{2,0,1:T(8,128)(2,1)S(1)}, u32[]{:S(2)}, u32[]{:S(2)}) collective-permute-start(bf16[12,8,128]{2,0,1:T(8,128)(2,1)S(1)} %copy.78), channel_id=1, source_target_pairs={{2,0},{3,1},{4,2},{5,3},{6,4},{7,5},{8,6},{9,7},{10,8},{11,9},{12,... | collective-permute-start | bytes 73736 | tf_op jit(solution)/shard_map/ppermute | solution.py:17
  14.0 0.5 compare_and_fusion.7
  14.6 0.6 compare_and_fusion.5
  15.2 0.6 compare_and_fusion.6
  15.8 0.6 compare_and_fusion.9
  16.3 0.6 compare_and_fusion.2
  17.0 1.5 %reverse_select_fusion = (bf16[4,4,128,128]{3,2,1,0:T(8,128)(2,1)S(1)}, bf16[4,4,128,128]{3,2,1,0:T(8,128)(2,1)S(1)}) fusion(bf16[4,4,128,128]{3,2,1,0:T(8,128)(2,1)} %param.25, pred[]{:T(512)S(6)} %ge.100, bf16[4,4,128,128]{3,2,1,0:T(8,128)(2,1)} %param.19), kind=kLoop, calls=%fused_computation.100 | loop fusion | flops 524288 | bytes 2097153 | tf_op jit(solution)/shard_map/jit(_where)/select_n | solution.py:161
  18.8 0.5 copy-done.15
  19.3 0.2 copy-done.12
  19.6 0.3 copy-done.6
  20.2 0.2 fusion.138
  21.4 1.3 %select_convert_fusion = bf16[37,128,128]{2,1,0:T(8,128)(2,1)S(1)} fusion(bf16[144,37,128]{2,0,1:T(8,128)(2,1)S(1)} %slice_dynamic-update-slice_fusion, bf16[144,128,1]{1,0,2:T(8,128)(2,1)S(1)} %bitcast.211, pred[37]{0:T(512)(128)(4,1)S(1)} %copy-done.23), kind=kOutput, calls=%fused_computation.2 | convolution fusion | flops 178225152 | bytes 2613285 | tf_op jit(solution)/shard_map/krw,ko->rwo/dot_general | solution.py:88
  22.7 0.8 %copy.122 = bf16[37,1,128,128]{3,0,2,1:T(8,128)(2,1)S(1)} copy(bf16[37,1,128,128]{3,2,0,1:T(8,128)(2,1)S(1)} %bitcast.196) | data formatting | bytes 2424832
  23.5 0.2 pad.44.clone
  23.7 0.4 copy.84
  24.2 0.2 copy-done.22
  24.4 1.0 %fusion.49 = bf16[18,1,8,9,128]{4,2,3,0,1:T(8,128)(2,1)S(1)} fusion(bf16[3,3,128,128]{3,2,1,0:T(8,128)(2,1)S(1)} %get-tuple-element.16, bf16[37,1,7,2,128]{4,2,3,0,1:T(8,128)(2,1)S(1)} %slice.354, bf16[37,1,8,18,128]{4,2,3,0,1:T(8,128)(2,1)S(1)} %copy.84, pred[18]{0:T(512)(128)(4,1)S(1)} %copy-done.22, pred[8,9]{0,1:T(8,128)(4,1)S(1)} %copy-done.24), kind=kOutput, calls=%fused_computation.81 | convolution fusion | flops 388079616 | bytes 2123354 | tf_op jit(solution)/shard_map/conv_general_dilated | solution.py:52
  25.5 0.9 %fusion.84 = bf16[16,8,9,128]{3,1,2,0:T(8,128)(2,1)S(1)} fusion(bf16[3,3,128,128]{3,2,1,0:T(8,128)(2,1)S(1)} %get-tuple-element.17, bf16[18,1,7,1,128]{4,2,3,0,1:T(8,128)(2,1)S(1)} %get-tuple-element.30, bf16[18,1,7,1,128]{4,2,3,0,1:T(8,128)(2,1)S(1)} %get-tuple-element.29, bf16[18,1,8,9,128]{4,2,3,0,1:T(8,128)(2,1)S(1)} %fusion.49, ...), kind=kOutput, calls=%fused_computation.123 | convolution fusion | flops 342798336 | bytes 986200 | tf_op jit(solution)/shard_map/conv_general_dilated | solution.py:52
  26.6 1.1 %fusion.121 = f32[28,8,16,128]{3,1,2,0:T(8,128)S(1)} fusion(bf16[4,4,128,128]{3,2,1,0:T(8,128)(2,1)S(1)} %get-tuple-element.18, bf16[16,1,7,1,128]{4,2,3,0,1:T(8,128)(2,1)S(1)} %get-tuple-element.32, bf16[16,1,7,1,128]{4,2,3,0,1:T(8,128)(2,1)S(1)} %get-tuple-element.31, bf16[16,1,8,8,128]{4,2,3,0,1:T(8,128)(2,1)S(1)} %copy.87), kind=kOutput, calls=%fused_computation.148 | convolution fusion | flops 471400448 | bytes 2678784 | tf_op jit(solution)/shard_map/conv_general_dilated | solution.py:52
  27.7 0.3 copy.90
  28.1 0.3 fusion.3
  28.4 0.6 copy.123
  29.0 0.2 pad.50.clone
  29.2 0.4 copy.93
  29.6 0.2 copy-done.18
  29.9 2.4 %convolution_select_fusion = f32[26,8,17,128]{3,1,2,0:T(8,128)S(1)} fusion(bf16[3,3,128,128]{3,2,1,0:T(8,128)(2,1)S(1)} %get-tuple-element.19, bf16[28,1,7,2,128]{4,2,3,0,1:T(8,128)(2,1)S(1)} %slice.360, bf16[28,1,8,17,128]{4,2,3,0,1:T(8,128)(2,1)S(1)} %copy.93, pred[8,17]{0,1:T(8,128)(4,1)S(1)} %copy-done.18), kind=kOutput, calls=%fused_computation.25 | convolution fusion | flops 1046530048 | bytes 3180680 | tf_op jit(solution)/shard_map/conv_general_dilated | solution.py:52
  32.2 0.6 copy.94
  32.8 0.2 slice.361
  33.0 0.5 copy-done.20
  33.5 1.3 %fusion.36 = f32[36,26,128]{2,0,1:T(8,128)S(1)} fusion(f32[26,1,128,128]{3,0,2,1:T(8,128)S(1)} %slice.361, pred[26]{0:T(512)(128)(4,1)S(1)} %copy-done.20, bf16[36,128]{1,0:T(8,128)(2,1)S(1)} %select_n.141), kind=kOutput, calls=%fused_computation.55 | convolution fusion | flops 33226752 | bytes 2192410 | tf_op jit(solution)/shard_map/tc,rwc->trw/dot_general | solution.py:120
  34.8 0.2 fusion.307
  36.8 0.6 fusion.315
  37.4 0.8 %select_convert_fusion.3 = bf16[21,128,128]{2,1,0:T(8,128)(2,1)S(1)} fusion(f32[21,128,128]{2,1,0:T(8,128)S(1)} %fusion.315, bf16[144,21,128]{2,0,1:T(8,128)(2,1)S(1)} %slice_dynamic-update-slice_fusion.18, bf16[144,128,1]{1,0,2:T(8,128)(2,1)S(1)} %bitcast.212, pred[21]{0:T(512)(128)(4,1)S(1)} %copy-done.19), kind=kOutput, calls=%fused_computation.29 | convolution fusion | flops 101498880 | bytes 2875413 | tf_op jit(solution)/shard_map/krw,ko->rwo/dot_general | solution.py:88
  38.1 0.5 copy.124
  38.6 0.2 pad.52.clone
  38.8 0.2 copy.98
  39.0 0.6 fusion.116
  39.7 0.6 fusion.150
  40.4 0.6 fusion.191
  41.6 1.0 %convolution_select_fusion.2 = f32[10,8,17,128]{3,1,2,0:T(8,128)S(1)} fusion(bf16[3,3,128,128]{3,2,1,0:T(8,128)(2,1)S(1)} %get-tuple-element.24, bf16[12,1,7,2,128]{4,2,3,0,1:T(8,128)(2,1)S(1)} %slice.388, bf16[12,1,8,17,128]{4,2,3,0,1:T(8,128)(2,1)S(1)} %copy.106, pred[8,17]{0,1:T(8,128)(4,1)S(1)} %copy-done.18), kind=kOutput, calls=%fused_computation.31 | convolution fusion | flops 402655232 | bytes 1452168 | tf_op jit(solution)/shard_map/conv_general_dilated | solution.py:52
  42.6 0.2 copy.107
  42.8 0.4 fusion.134
  43.3 0.3 copy-done.13
  43.7 8.4 %collective-permute-start.4 = (bf16[4,8,128]{2,0,1:T(4,128)(2,1)S(1)}, bf16[4,8,128]{2,0,1:T(4,128)(2,1)S(1)}, u32[]{:S(2)}, u32[]{:S(2)}) collective-permute-start(bf16[4,8,128]{2,0,1:T(4,128)(2,1)S(1)} %get-tuple-element.25), channel_id=1, source_target_pairs={{0,1},{1,2},{2,3},{3,4},{4,5},{5,6},{6,7},{7,8},{8,9},{9,10},{10,1... | collective-permute-start | bytes 24584 | tf_op jit(solution)/shard_map/ppermute | solution.py:17
  52.1 2.1 %collective-permute-start.5 = (bf16[4,8,128]{2,0,1:T(4,128)(2,1)S(1)}, bf16[4,8,128]{2,0,1:T(4,128)(2,1)S(1)}, u32[]{:S(2)}, u32[]{:S(2)}) collective-permute-start(bf16[4,8,128]{2,0,1:T(4,128)(2,1)S(1)} %get-tuple-element.25), channel_id=1, source_target_pairs={{1,0},{2,1},{3,2},{4,3},{5,4},{6,5},{7,6},{8,7},{9,8},{10,9},{11,1... | collective-permute-start | bytes 24584 | tf_op jit(solution)/shard_map/ppermute | solution.py:17
  54.3 4.9 %collective-permute-done.5 = bf16[4,8,128]{2,0,1:T(4,128)(2,1)S(1)} collective-permute-done((bf16[4,8,128]{2,0,1:T(4,128)(2,1)S(1)}, bf16[4,8,128]{2,0,1:T(4,128)(2,1)S(1)}, u32[]{:S(2)}, u32[]{:S(2)}) %collective-permute-start.5) | collective-permute-done | bytes 8224 | tf_op jit(solution)/shard_map/ppermute | solution.py:17
  60.1 0.8 %select_convert_fusion.2 = bf16[21,128,128]{2,1,0:T(8,128)(2,1)S(1)} fusion(f32[21,128,128]{2,1,0:T(8,128)S(1)} %fusion.315, bf16[144,21,128]{2,0,1:T(8,128)(2,1)S(1)} %slice_dynamic-update-slice_fusion.9, bf16[144,128,1]{1,0,2:T(8,128)(2,1)S(1)} %bitcast.213, pred[21]{0:T(512)(128)(4,1)S(1)} %copy-done.19), kind=kOutput, calls=%fused_computation.28 | convolution fusion | flops 101498880 | bytes 2875413 | tf_op jit(solution)/shard_map/krw,ko->rwo/dot_general | solution.py:88
  60.9 0.5 copy.125
  61.5 0.2 copy.110
  61.8 0.5 copy-done.9
  62.3 0.6 fusion.108
  63.0 0.3 copy-done.11
  63.3 0.5 fusion.160
  63.9 0.4 copy-done.1
  64.3 0.6 fusion.196
  65.5 1.0 %convolution_select_fusion.1 = f32[10,8,17,128]{3,1,2,0:T(8,128)S(1)} fusion(bf16[3,3,128,128]{3,2,1,0:T(8,128)(2,1)S(1)} %get-tuple-element.24, bf16[12,1,7,2,128]{4,2,3,0,1:T(8,128)(2,1)S(1)} %slice.409, bf16[12,1,8,17,128]{4,2,3,0,1:T(8,128)(2,1)S(1)} %copy.118, pred[8,17]{0,1:T(8,128)(4,1)S(1)} %copy-done.18), kind=kOutput, calls=%fused_computation.30 | convolution fusion | flops 402655232 | bytes 1452168 | tf_op jit(solution)/shard_map/conv_general_dilated | solution.py:52
  66.5 0.2 copy.119
  66.7 0.4 fusion.135
  67.3 0.6 copy.120
  (140 shorter events, 6.3 us)
Async XLA Ops:
  0.0 18.5 %copy-start.3 = (bf16[3,3,128,128]{3,2,1,0:T(8,128)(2,1)S(1)}, bf16[3,3,128,128]{3,2,1,0:T(8,128)(2,1)}, u32[]{:S(2)}) copy-start(bf16[3,3,128,128]{3,2,1,0:T(8,128)(2,1)} %param.20) | copy-start | bytes 884740
  0.0 18.5 %copy-start.2 = (bf16[3,3,128,128]{3,2,1,0:T(8,128)(2,1)S(1)}, bf16[3,3,128,128]{3,2,1,0:T(8,128)(2,1)}, u32[]{:S(2)}) copy-start(bf16[3,3,128,128]{3,2,1,0:T(8,128)(2,1)} %param.23) | copy-start | bytes 884740
  1.6 18.5 %collective-permute-start.1 = (bf16[16,8,128]{2,0,1:T(8,128)(2,1)S(1)}, bf16[16,8,128]{2,0,1:T(8,128)(2,1)S(1)}, u32[]{:S(2)}, u32[]{:S(2)}) collective-permute-start(bf16[16,8,128]{2,0,1:T(8,128)(2,1)S(1)} %pad_maximum_fusion.2), channel_id=1, source_target_pairs={{0,1},{1,2},{2,3},{3,4},{4,5},{5,6},{6,7},{7,8},{8,9},{9,10},{10,1... | collective-permute-start | bytes 98312 | tf_op jit(solution)/shard_map/ppermute | solution.py:17
  6.8 13.3 %collective-permute-start.2 = (bf16[16,8,128]{2,0,1:T(8,128)(2,1)S(1)}, bf16[16,8,128]{2,0,1:T(8,128)(2,1)S(1)}, u32[]{:S(2)}, u32[]{:S(2)}) collective-permute-start(bf16[16,8,128]{2,0,1:T(8,128)(2,1)S(1)} %pad_maximum_fusion.2), channel_id=1, source_target_pairs={{1,0},{2,1},{3,2},{4,3},{5,4},{6,5},{7,6},{8,7},{9,8},{10,9},{11,1... | collective-permute-start | bytes 98312 | tf_op jit(solution)/shard_map/ppermute | solution.py:17
  8.7 11.5 %collective-permute-start = (bf16[12,8,128]{2,0,1:T(8,128)(2,1)S(1)}, bf16[12,8,128]{2,0,1:T(8,128)(2,1)S(1)}, u32[]{:S(2)}, u32[]{:S(2)}) collective-permute-start(bf16[12,8,128]{2,0,1:T(8,128)(2,1)S(1)} %copy.78), channel_id=1, source_target_pairs={{0,2},{1,3},{2,4},{3,5},{4,6},{5,7},{6,8},{7,9},{8,10},{9,11},{10,... | collective-permute-start | bytes 73736 | tf_op jit(solution)/shard_map/ppermute | solution.py:17
  11.6 8.6 %collective-permute-start.3 = (bf16[12,8,128]{2,0,1:T(8,128)(2,1)S(1)}, bf16[12,8,128]{2,0,1:T(8,128)(2,1)S(1)}, u32[]{:S(2)}, u32[]{:S(2)}) collective-permute-start(bf16[12,8,128]{2,0,1:T(8,128)(2,1)S(1)} %copy.78), channel_id=1, source_target_pairs={{2,0},{3,1},{4,2},{5,3},{6,4},{7,5},{8,6},{9,7},{10,8},{11,9},{12,... | collective-permute-start | bytes 73736 | tf_op jit(solution)/shard_map/ppermute | solution.py:17
  17.0 1.7 %copy-start.4 = (bf16[3,3,128,128]{3,2,1,0:T(8,128)(2,1)S(1)}, bf16[3,3,128,128]{3,2,1,0:T(8,128)(2,1)}, u32[]{:S(2)}) copy-start(bf16[3,3,128,128]{3,2,1,0:T(8,128)(2,1)} %param.18) | copy-start | bytes 884740
  17.0 1.7 %copy-start.5 = (bf16[3,3,128,128]{3,2,1,0:T(8,128)(2,1)S(1)}, bf16[3,3,128,128]{3,2,1,0:T(8,128)(2,1)}, u32[]{:S(2)}) copy-start(bf16[3,3,128,128]{3,2,1,0:T(8,128)(2,1)} %param.17) | copy-start | bytes 884740
  18.5 21.9 %copy-start = (bf16[4,4,128,128]{3,2,1,0:T(8,128)(2,1)}, bf16[4,4,128,128]{3,2,1,0:T(8,128)(2,1)S(1)}, u32[]{:S(2)}) copy-start(bf16[4,4,128,128]{3,2,1,0:T(8,128)(2,1)S(1)} %get-tuple-element.23) | copy-start | bytes 1572868
  18.5 0.7 %copy-start.15 = (bf16[3,3,4,128]{3,2,1,0:T(4,128)(2,1)S(1)}, bf16[3,3,4,128]{3,2,1,0:T(4,128)(2,1)}, u32[]{:S(2)}) copy-start(bf16[3,3,4,128]{3,2,1,0:T(4,128)(2,1)} %param.27) | copy-start | bytes 27652
  18.5 0.8 %copy-start.16 = (bf16[3,3,4,128]{3,2,1,0:T(4,128)(2,1)S(1)}, bf16[3,3,4,128]{3,2,1,0:T(4,128)(2,1)}, u32[]{:S(2)}) copy-start(bf16[3,3,4,128]{3,2,1,0:T(4,128)(2,1)} %param.21) | copy-start | bytes 27652
  18.6 1.0 %copy-start.12 = (bf16[3,3,20,128]{3,2,1,0:T(8,128)(2,1)S(1)}, bf16[3,3,20,128]{3,2,1,0:T(8,128)(2,1)}, u32[]{:S(2)}) copy-start(bf16[3,3,20,128]{3,2,1,0:T(8,128)(2,1)} %param.22) | copy-start | bytes 138244
  18.6 1.0 %copy-start.17 = (pred[16]{0:T(512)(128)(4,1)S(1)}, pred[16]{0:T(512)(128)(4,1)}, u32[]{:S(2)}) copy-start(pred[16]{0:T(512)(128)(4,1)} %constant.53.clone.1) | copy-start | bytes 52
  18.6 1.3 %copy-start.6 = (bf16[3,3,128,128]{3,2,1,0:T(8,128)(2,1)S(1)}, bf16[3,3,128,128]{3,2,1,0:T(8,128)(2,1)}, u32[]{:S(2)}) copy-start(bf16[3,3,128,128]{3,2,1,0:T(8,128)(2,1)} %param.26) | copy-start | bytes 884740
  18.6 1.4 %copy-start.7 = (bf16[3,3,128,128]{3,2,1,0:T(8,128)(2,1)S(1)}, bf16[3,3,128,128]{3,2,1,0:T(8,128)(2,1)}, u32[]{:S(2)}) copy-start(bf16[3,3,128,128]{3,2,1,0:T(8,128)(2,1)} %param.24) | copy-start | bytes 884740
  18.7 20.3 %copy-start.8 = (bf16[3,3,128,128]{3,2,1,0:T(8,128)(2,1)}, bf16[3,3,128,128]{3,2,1,0:T(8,128)(2,1)S(1)}, u32[]{:S(2)}) copy-start(bf16[3,3,128,128]{3,2,1,0:T(8,128)(2,1)S(1)} %get-tuple-element.21) | copy-start | bytes 884740
  18.7 1.4 %copy-start.14 = (bf16[3,3,12,128]{3,2,1,0:T(8,128)(2,1)S(1)}, bf16[3,3,12,128]{3,2,1,0:T(8,128)(2,1)}, u32[]{:S(2)}) copy-start(bf16[3,3,12,128]{3,2,1,0:T(8,128)(2,1)} %param.16) | copy-start | bytes 82948
  20.0 19.7 %copy-start.10 = (bf16[3,3,128,128]{3,2,1,0:T(8,128)(2,1)}, bf16[3,3,128,128]{3,2,1,0:T(8,128)(2,1)S(1)}, u32[]{:S(2)}) copy-start(bf16[3,3,128,128]{3,2,1,0:T(8,128)(2,1)S(1)} %get-tuple-element.22) | copy-start | bytes 884740
  20.4 1.0 %copy-start.23 = (pred[37]{0:T(512)(128)(4,1)S(1)}, pred[37]{0:T(512)(128)(4,1)}, u32[]{:S(2)}) copy-start(pred[37]{0:T(512)(128)(4,1)} %compare_and_fusion.7) | copy-start | bytes 115
  23.7 0.7 copy-start.22
  23.7 0.7 %copy-start.24 = (pred[8,9]{0,1:T(8,128)(4,1)S(1)}, pred[8,9]{0,1:T(8,128)(4,1)}, u32[]{:S(2)}) copy-start(pred[8,9]{0,1:T(8,128)(4,1)} %constant.189) | copy-start | bytes 220
  24.4 1.1 %copy-start.21 = (pred[16]{0:T(512)(128)(4,1)S(1)}, pred[16]{0:T(512)(128)(4,1)}, u32[]{:S(2)}) copy-start(pred[16]{0:T(512)(128)(4,1)} %compare_and_fusion.6) | copy-start | bytes 52
  29.2 0.7 %copy-start.18 = (pred[8,17]{0,1:T(8,128)(4,1)S(1)}, pred[8,17]{0,1:T(8,128)(4,1)}, u32[]{:S(2)}) copy-start(pred[8,17]{0,1:T(8,128)(4,1)} %constant.188) | copy-start | bytes 412
  32.8 0.7 copy-start.20
  36.5 0.9 %copy-start.19 = (pred[21]{0:T(512)(128)(4,1)S(1)}, pred[21]{0:T(512)(128)(4,1)}, u32[]{:S(2)}) copy-start(pred[21]{0:T(512)(128)(4,1)} %compare_and_fusion.2) | copy-start | bytes 67
  42.8 0.7 %copy-start.13 = (f32[1,4,8,128]{3,2,1,0:T(8,128)S(1)}, f32[1,4,8,128]{3,2,1,0:T(8,128)}, u32[]{:S(2)}) copy-start(f32[1,4,8,128]{3,2,1,0:T(8,128)} %param.15) | copy-start | bytes 49156
  43.7 10.6 %collective-permute-start.4 = (bf16[4,8,128]{2,0,1:T(4,128)(2,1)S(1)}, bf16[4,8,128]{2,0,1:T(4,128)(2,1)S(1)}, u32[]{:S(2)}, u32[]{:S(2)}) collective-permute-start(bf16[4,8,128]{2,0,1:T(4,128)(2,1)S(1)} %get-tuple-element.25), channel_id=1, source_target_pairs={{0,1},{1,2},{2,3},{3,4},{4,5},{5,6},{6,7},{7,8},{8,9},{9,10},{10,1... | collective-permute-start | bytes 24584 | tf_op jit(solution)/shard_map/ppermute | solution.py:17
  52.1 7.1 %collective-permute-start.5 = (bf16[4,8,128]{2,0,1:T(4,128)(2,1)S(1)}, bf16[4,8,128]{2,0,1:T(4,128)(2,1)S(1)}, u32[]{:S(2)}, u32[]{:S(2)}) collective-permute-start(bf16[4,8,128]{2,0,1:T(4,128)(2,1)S(1)} %get-tuple-element.25), channel_id=1, source_target_pairs={{1,0},{2,1},{3,2},{4,3},{5,4},{6,5},{7,6},{8,7},{9,8},{10,9},{11,1... | collective-permute-start | bytes 24584 | tf_op jit(solution)/shard_map/ppermute | solution.py:17
  61.3 1.0 %copy-start.9 = (bf16[3,3,128,128]{3,2,1,0:T(8,128)(2,1)S(1)}, bf16[3,3,128,128]{3,2,1,0:T(8,128)(2,1)}, u32[]{:S(2)}) copy-start(bf16[3,3,128,128]{3,2,1,0:T(8,128)(2,1)} %copy-done.8) | copy-start | bytes 884740
  62.3 1.0 %copy-start.11 = (bf16[3,3,128,128]{3,2,1,0:T(8,128)(2,1)S(1)}, bf16[3,3,128,128]{3,2,1,0:T(8,128)(2,1)}, u32[]{:S(2)}) copy-start(bf16[3,3,128,128]{3,2,1,0:T(8,128)(2,1)} %copy-done.10) | copy-start | bytes 884740
  63.3 1.0 %copy-start.1 = (bf16[4,4,128,128]{3,2,1,0:T(8,128)(2,1)S(1)}, bf16[4,4,128,128]{3,2,1,0:T(8,128)(2,1)}, u32[]{:S(2)}) copy-start(bf16[4,4,128,128]{3,2,1,0:T(8,128)(2,1)} %copy-done) | copy-start | bytes 1572868

commit v3 on v1

--- a/solution.py
+++ b/solution.py
@@ -194,11 +194,7 @@
     cond_near = near_wide[noise_count:]
     reg_mean = mean_wide[:, dif_halo : dif_halo + rows]
 
-    dif_top_lo, dif_top_hi = windows(0, rows)[6:]
     fixed_in = jnp.concatenate([cond_near, mean_input], axis=0)
-    fixed_top = conv_in(
-        fixed_in, -dif_halo, dif_top_lo, dif_top_hi, dif_in[:, :, noise_count:]
-    )
     field_in = near_wide[:noise_count]
     for step_index in range(STEPS):
         in_gain, skip_gain, out_gain, step_gain = gains[step_index]
@@ -206,9 +202,8 @@
             field_in = halo_rows(
                 (in_gain * residual_field).astype(jnp.bfloat16), 1, dif_halo, dif_halo
             )
-        network = unet(
-            field_in, -dif_halo, 0, rows, dif_weights, base, grid_rows, top_extra=fixed_top
-        )
+        inputs = jnp.concatenate([field_in, fixed_in], axis=0)
+        network = unet(inputs, -dif_halo, 0, rows, dif_weights, base, grid_rows)
         denoised = skip_gain * residual_field + out_gain * network
         residual_field = residual_field + step_gain * (residual_field - denoised)
     return (reg_mean + residual_field)[None]

time: 68.8 us -> 65 us (0.945)
  the two profiles are of different devices: /device:TPU:351 before, /device:TPU:415 now
where the time goes in v3:
time: 65 us; the launch traced here: 64.3 us
  starting transfers between devices  22.1 us (34%)
  local copies, waits for them, and re-layouts  17.1 us (26%)
  matrix products  15.7 us (24%)
  waiting for transfers between devices  5.91 us (9%)
  other arithmetic  2.55 us (4%)
  between operations  0.99 us (2%)
    ppermute x6, starting transfers between devices, from_tile(): return lax.ppermute(values, 'tile', pairs)  22.1 us
    conv_general_dilated x12, matrix products, conv(): lax.conv_general_dilated(lhs, rhs, window_strides=strides, padding=paddin...  11.1 us
    unnamed x51, local copies, waits for them, and re-layouts  8.56 us
    ppermute x6, waiting for transfers between devices, from_tile(): return lax.ppermute(values, 'tile', pairs)  5.91 us
    dot_general x3, matrix products, conv_in(): jnp.einsum('krw,ko->rwo', patches, flat, preferred_element_type=jnp.float32)  3.15 us
    conv_general_dilated x17, local copies, waits for them, and re-layouts, conv(): lax.conv_general_dilated(lhs, rhs, window_strides=strides, padding=paddin...  2.34 us
    pad x2, local copies, waits for them, and re-layouts, conv_in(): weight = jnp.pad(weight, ((0, 0), (0, 0), (0, extra), (0, 0)))  1.61 us
    dot_general x3, matrix products, conv_out(): jnp.einsum('tc,rwc->trw', flat, refined, preferred_element_type=jnp.float32)  1.49 us
  transfers between devices with their start and end apart: 6, of which 2 were waited for; matrix products, arithmetic and copies ran while one was open for 5% of the time, Pallas kernels for 0%

profile of v3, /device:TPU:415, one launch (start us, length us, event | category | flops | bytes accessed | tf_op | source)
XLA Modules:
  0.0 64.3 jit_solution(10979812430985575858)
XLA Ops:
  0.0 0.8 %copy.35 = bf16[12,8,128]{2,0,1:T(8,128)(2,1)S(1)} copy(bf16[12,8,128]{2,1,0:T(8,128)(2,1)} %param.14) | data formatting | bytes 49152 | tf_op args[0]
  0.8 0.7 %fusion.245 = bf16[4,8,128]{2,0,1:T(4,128)(2,1)S(1)} fusion(f32[1,4,8,128]{3,2,1,0:T(8,128)} %param.15), kind=kLoop, calls=%fused_computation.295 | loop fusion | flops 8192 | bytes 24576 | tf_op jit(solution)/shard_map/convert_element_type | solution.py:173
  1.6 5.2 %collective-permute-start.1 = (bf16[16,8,128]{2,0,1:T(8,128)(2,1)S(1)}, bf16[16,8,128]{2,0,1:T(8,128)(2,1)S(1)}, u32[]{:S(2)}, u32[]{:S(2)}) collective-permute-start(bf16[16,8,128]{2,0,1:T(8,128)(2,1)S(1)} %pad_maximum_fusion.3), channel_id=1, source_target_pairs={{0,1},{1,2},{2,3},{3,4},{4,5},{5,6},{6,7},{7,8},{8,9},{9,10},{10,1... | collective-permute-start | bytes 98312 | tf_op jit(solution)/shard_map/ppermute | solution.py:17
  6.8 1.9 %collective-permute-start.2 = (bf16[16,8,128]{2,0,1:T(8,128)(2,1)S(1)}, bf16[16,8,128]{2,0,1:T(8,128)(2,1)S(1)}, u32[]{:S(2)}, u32[]{:S(2)}) collective-permute-start(bf16[16,8,128]{2,0,1:T(8,128)(2,1)S(1)} %pad_maximum_fusion.3), channel_id=1, source_target_pairs={{1,0},{2,1},{3,2},{4,3},{5,4},{6,5},{7,6},{8,7},{9,8},{10,9},{11,1... | collective-permute-start | bytes 98312 | tf_op jit(solution)/shard_map/ppermute | solution.py:17
  8.7 2.8 %collective-permute-start = (bf16[12,8,128]{2,0,1:T(8,128)(2,1)S(1)}, bf16[12,8,128]{2,0,1:T(8,128)(2,1)S(1)}, u32[]{:S(2)}, u32[]{:S(2)}) collective-permute-start(bf16[12,8,128]{2,0,1:T(8,128)(2,1)S(1)} %copy.35), channel_id=1, source_target_pairs={{0,2},{1,3},{2,4},{3,5},{4,6},{5,7},{6,8},{7,9},{8,10},{9,11},{10,... | collective-permute-start | bytes 73736 | tf_op jit(solution)/shard_map/ppermute | solution.py:17
  11.6 2.5 %collective-permute-start.3 = (bf16[12,8,128]{2,0,1:T(8,128)(2,1)S(1)}, bf16[12,8,128]{2,0,1:T(8,128)(2,1)S(1)}, u32[]{:S(2)}, u32[]{:S(2)}) collective-permute-start(bf16[12,8,128]{2,0,1:T(8,128)(2,1)S(1)} %copy.35), channel_id=1, source_target_pairs={{2,0},{3,1},{4,2},{5,3},{6,4},{7,5},{8,6},{9,7},{10,8},{11,9},{12,... | collective-permute-start | bytes 73736 | tf_op jit(solution)/shard_map/ppermute | solution.py:17
  14.2 0.7 %reshape.269 = bf16[36,128,1]{1,0,2:T(8,128)(2,1)S(1)} reshape(bf16[3,3,4,128]{3,2,1,0:T(4,128)(2,1)} %param.21) | data formatting | bytes 18432 | tf_op jit(solution)/shard_map/reshape | solution.py:120
  14.9 0.8 %pad.32 = bf16[3,3,16,128]{3,2,1,0:T(8,128)(2,1)S(1)} pad(bf16[3,3,12,128]{3,2,1,0:T(8,128)(2,1)} %param.16, bf16[]{:T(256)} %constant.42.clone.1), padding=0_0x0_0x0_4x0_0 | pad | bytes 64514 | tf_op jit(solution)/shard_map/jit(_pad)/pad | solution.py:80
  15.7 0.8 %pad.35 = bf16[3,3,32,128]{3,2,1,0:T(8,128)(2,1)S(1)} pad(bf16[3,3,20,128]{3,2,1,0:T(8,128)(2,1)} %param.22, bf16[]{:T(256)} %constant.42.clone.1), padding=0_0x0_0x0_12x0_0 | pad | bytes 119810 | tf_op jit(solution)/shard_map/jit(_pad)/pad | solution.py:80
  16.6 0.7 %reshape.271 = bf16[36,128,1]{1,0,2:T(8,128)(2,1)S(1)} reshape(bf16[3,3,4,128]{3,2,1,0:T(4,128)(2,1)} %param.27) | data formatting | bytes 18432 | tf_op jit(solution)/shard_map/reshape | solution.py:120
  17.4 1.0 %collective-permute-done.3 = bf16[12,8,128]{2,0,1:T(8,128)(2,1)S(1)} collective-permute-done((bf16[12,8,128]{2,0,1:T(8,128)(2,1)S(1)}, bf16[12,8,128]{2,0,1:T(8,128)(2,1)S(1)}, u32[]{:S(2)}, u32[]{:S(2)}) %collective-permute-start.3) | collective-permute-done | bytes 24608 | tf_op jit(solution)/shard_map/ppermute | solution.py:17
  18.3 0.2 fusion.154
  19.5 1.3 %select_convert_fusion = bf16[37,128,128]{2,1,0:T(8,128)(2,1)S(1)} fusion(bf16[144,37,128]{2,0,1:T(8,128)(2,1)S(1)} %slice_dynamic-update-slice_fusion.18, bf16[144,128,1]{1,0,2:T(8,128)(2,1)S(1)} %bitcast.202, pred[37]{0:T(512)(128)(4,1)S(1)} %compare_and_fusion.7), kind=kOutput, calls=%fused_computation.2 | convolution fusion | flops 178225152 | bytes 2613285 | tf_op jit(solution)/shard_map/krw,ko->rwo/dot_general | solution.py:88
  20.8 0.8 %copy.79 = bf16[37,1,128,128]{3,0,2,1:T(8,128)(2,1)S(1)} copy(bf16[37,1,128,128]{3,2,0,1:T(8,128)(2,1)S(1)} %bitcast.186) | data formatting | bytes 2424832
  21.6 0.2 pad.39.clone
  21.8 0.4 copy.41
  22.3 0.5 copy-done.3
  22.8 1.0 %fusion.59 = bf16[18,1,8,9,128]{4,2,3,0,1:T(8,128)(2,1)S(1)} fusion(bf16[3,3,128,128]{3,2,1,0:T(8,128)(2,1)S(1)} %copy-done.3, bf16[37,1,7,2,128]{4,2,3,0,1:T(8,128)(2,1)S(1)} %slice.297, bf16[37,1,8,18,128]{4,2,3,0,1:T(8,128)(2,1)S(1)} %copy.41, pred[18]{0:T(512)(128)(4,1)S(1)} %compare_and_fusion.5, pred[8,9]{0,1:T(8,128)(4,1)S(1)} %copy-done.10), kind=kOutput, calls=%fused_computation.96 | convolution fusion | flops 388079616 | bytes 2123354 | tf_op jit(solution)/shard_map/conv_general_dilated | solution.py:52
  23.9 0.9 %fusion.94 = bf16[16,8,9,128]{3,1,2,0:T(8,128)(2,1)S(1)} fusion(bf16[3,3,128,128]{3,2,1,0:T(8,128)(2,1)S(1)} %copy-done.4, bf16[18,1,7,1,128]{4,2,3,0,1:T(8,128)(2,1)S(1)} %get-tuple-element.10, bf16[18,1,7,1,128]{4,2,3,0,1:T(8,128)(2,1)S(1)} %get-tuple-element.9, bf16[18,1,8,9,128]{4,2,3,0,1:T(8,128)(2,1)S(1)} %fusion.59, ...), kind=kOutput, calls=%fused_computation.130 | convolution fusion | flops 342798336 | bytes 986200 | tf_op jit(solution)/shard_map/conv_general_dilated | solution.py:52
  25.0 1.1 %fusion.139 = f32[28,8,16,128]{3,1,2,0:T(8,128)S(1)} fusion(bf16[4,4,128,128]{3,2,1,0:T(8,128)(2,1)S(1)} %copy-done, bf16[16,1,7,1,128]{4,2,3,0,1:T(8,128)(2,1)S(1)} %get-tuple-element.12, bf16[16,1,7,1,128]{4,2,3,0,1:T(8,128)(2,1)S(1)} %get-tuple-element.11, bf16[16,1,8,8,128]{4,2,3,0,1:T(8,128)(2,1)S(1)} %copy.44), kind=kOutput, calls=%fused_computation.162 | convolution fusion | flops 471400448 | bytes 2678784 | tf_op jit(solution)/shard_map/conv_general_dilated | solution.py:52
  26.1 0.3 copy.47
  26.5 0.3 fusion.3
  26.7 0.6 copy.80
  27.4 0.2 pad.45.clone
  27.6 0.4 copy.50
  28.0 0.5 copy-done.5
  28.5 2.4 %select_convert_fusion.1 = bf16[26,8,17,128]{3,1,2,0:T(8,128)(2,1)S(1)} fusion(bf16[3,3,128,128]{3,2,1,0:T(8,128)(2,1)S(1)} %copy-done.5, bf16[28,1,7,2,128]{4,2,3,0,1:T(8,128)(2,1)S(1)} %slice.303, bf16[28,1,8,17,128]{4,2,3,0,1:T(8,128)(2,1)S(1)} %copy.50, pred[26]{0:T(512)(128)(4,1)S(1)} %compare_and_fusion.9, pred[8,17]{0,1:T(8,128)(4,1)S(1)} %copy-done.9), kind=kOutput, calls=%fused_computation.14 | convolution fusion | flops 1049245696 | bytes 2275490 | tf_op jit(solution)/shard_map/conv_general_dilated | solution.py:52
  31.0 0.2 copy.51
  31.3 0.8 %convolution_bitcast_fusion = f32[36,26,128]{2,0,1:T(8,128)S(1)} fusion(bf16[36,128,1]{1,0,2:T(8,128)(2,1)S(1)} %reshape.269, bf16[26,1,128,128]{3,0,2,1:T(8,128)(2,1)S(1)} %slice.304), kind=kOutput, calls=%fused_computation.29 | convolution fusion | flops 30670848 | bytes 1340416 | tf_op jit(solution)/shard_map/tc,rwc->trw/dot_general | solution.py:121
  32.1 0.2 fusion.290
  32.3 0.2 fusion.107
  32.6 0.1 slice_dynamic-update-slice_fusion.16
  32.7 0.1 slice_dynamic-update-slice_fusion.15
  33.6 0.9 %select_convert_fusion.3 = bf16[21,128,128]{2,1,0:T(8,128)(2,1)S(1)} fusion(bf16[288,21,128]{2,0,1:T(8,128)(2,1)S(1)} %slice_dynamic-update-slice_fusion.9, bf16[288,128,1]{1,0,2:T(8,128)(2,1)S(1)} %bitcast.200, pred[21]{0:T(512)(128)(4,1)S(1)} %compare_and_fusion.2), kind=kOutput, calls=%fused_computation.25 | convolution fusion | flops 200245248 | bytes 2310165 | tf_op jit(solution)/shard_map/krw,ko->rwo/dot_general | solution.py:88
  34.5 0.5 copy.81
  35.0 0.2 pad.47.clone
  35.1 0.2 copy.55
  35.4 0.5 copy-done.6
  35.9 0.6 fusion.134
  36.6 0.3 copy-done.7
  36.9 0.5 fusion.166
  37.6 0.4 copy-done.2
  37.9 0.6 fusion.195
  38.9 0.2 reshape.185
  39.2 0.6 copy-done.8
  39.8 1.0 %select_convert_fusion.5 = bf16[10,8,17,128]{3,1,2,0:T(8,128)(2,1)S(1)} fusion(bf16[3,3,128,128]{3,2,1,0:T(8,128)(2,1)S(1)} %copy-done.8, bf16[12,1,7,2,128]{4,2,3,0,1:T(8,128)(2,1)S(1)} %slice.325, bf16[12,1,8,17,128]{4,2,3,0,1:T(8,128)(2,1)S(1)} %copy.63, pred[10]{0:T(512)(128)(4,1)S(1)} %compare_and_fusion.4, pred[8,17]{0,1:T(8,128)(4,1)S(1)} %copy-done.9), kind=kOutput, calls=%fused_computation.93 | convolution fusion | flops 403699712 | bytes 1104018 | tf_op jit(solution)/shard_map/conv_general_dilated | solution.py:52
  41.1 0.3 convolution_bitcast_fusion.2
  41.7 7.5 %collective-permute-start.4 = (bf16[4,8,128]{2,0,1:T(4,128)(2,1)S(1)}, bf16[4,8,128]{2,0,1:T(4,128)(2,1)S(1)}, u32[]{:S(2)}, u32[]{:S(2)}) collective-permute-start(bf16[4,8,128]{2,0,1:T(4,128)(2,1)S(1)} %get-tuple-element.5), channel_id=1, source_target_pairs={{0,1},{1,2},{2,3},{3,4},{4,5},{5,6},{6,7},{7,8},{8,9},{9,10},{10,1... | collective-permute-start | bytes 24584 | tf_op jit(solution)/shard_map/ppermute | solution.py:17
  49.1 2.1 %collective-permute-start.5 = (bf16[4,8,128]{2,0,1:T(4,128)(2,1)S(1)}, bf16[4,8,128]{2,0,1:T(4,128)(2,1)S(1)}, u32[]{:S(2)}, u32[]{:S(2)}) collective-permute-start(bf16[4,8,128]{2,0,1:T(4,128)(2,1)S(1)} %get-tuple-element.5), channel_id=1, source_target_pairs={{1,0},{2,1},{3,2},{4,3},{5,4},{6,5},{7,6},{8,7},{9,8},{10,9},{11,1... | collective-permute-start | bytes 24584 | tf_op jit(solution)/shard_map/ppermute | solution.py:17
  51.3 4.9 %collective-permute-done.5 = bf16[4,8,128]{2,0,1:T(4,128)(2,1)S(1)} collective-permute-done((bf16[4,8,128]{2,0,1:T(4,128)(2,1)S(1)}, bf16[4,8,128]{2,0,1:T(4,128)(2,1)S(1)}, u32[]{:S(2)}, u32[]{:S(2)}) %collective-permute-start.5) | collective-permute-done | bytes 8224 | tf_op jit(solution)/shard_map/ppermute | solution.py:17
  56.2 0.3 fusion.117
  56.5 0.1 slice_dynamic-update-slice_fusion.7
  57.2 0.1 slice_dynamic-update-slice_fusion.1
  57.5 0.9 %select_convert_fusion.2 = bf16[21,128,128]{2,1,0:T(8,128)(2,1)S(1)} fusion(bf16[288,21,128]{2,0,1:T(8,128)(2,1)S(1)} %slice_dynamic-update-slice_fusion, bf16[288,128,1]{1,0,2:T(8,128)(2,1)S(1)} %bitcast.201, pred[21]{0:T(512)(128)(4,1)S(1)} %compare_and_fusion.2), kind=kOutput, calls=%fused_computation.24 | convolution fusion | flops 200245248 | bytes 2310165 | tf_op jit(solution)/shard_map/krw,ko->rwo/dot_general | solution.py:88
  58.4 0.5 copy.82
  58.9 0.2 pad.55.clone
  59.1 0.2 copy.67
  59.3 0.6 %fusion.126 = bf16[10,1,8,9,128]{4,2,3,0,1:T(8,128)(2,1)S(1)} fusion(bf16[3,3,128,128]{3,2,1,0:T(8,128)(2,1)S(1)} %copy-done.6, bf16[21,1,7,2,128]{4,2,3,0,1:T(8,128)(2,1)S(1)} %slice.340, bf16[21,1,8,18,128]{4,2,3,0,1:T(8,128)(2,1)S(1)} %copy.67, pred[10]{0:T(512)(128)(4,1)S(1)} %compare_and_fusion, pred[8,9]{0,1:T(8,128)(4,1)S(1)} %copy-done.10), kind=kOutput, calls=%fused_computation.156 | convolution fusion | flops 215654400 | bytes 1328722 | tf_op jit(solution)/shard_map/conv_general_dilated | solution.py:52
  60.0 0.6 fusion.176
  60.7 0.6 fusion.200
  61.7 0.2 reshape.209
  61.9 1.0 %select_convert_fusion.4 = bf16[10,8,17,128]{3,1,2,0:T(8,128)(2,1)S(1)} fusion(bf16[3,3,128,128]{3,2,1,0:T(8,128)(2,1)S(1)} %copy-done.8, bf16[12,1,7,2,128]{4,2,3,0,1:T(8,128)(2,1)S(1)} %slice.346, bf16[12,1,8,17,128]{4,2,3,0,1:T(8,128)(2,1)S(1)} %copy.75, pred[10]{0:T(512)(128)(4,1)S(1)} %compare_and_fusion.4, pred[8,17]{0,1:T(8,128)(4,1)S(1)} %copy-done.9), kind=kOutput, calls=%fused_computation.92 | convolution fusion | flops 403699712 | bytes 1104018 | tf_op jit(solution)/shard_map/conv_general_dilated | solution.py:52
  63.2 0.3 convolution_bitcast_fusion.1
  63.7 0.6 copy.77
  (95 shorter events, 4.9 us)
Async XLA Ops:
  0.0 25.0 %copy-start = (bf16[4,4,128,128]{3,2,1,0:T(8,128)(2,1)S(1)}, bf16[4,4,128,128]{3,2,1,0:T(8,128)(2,1)}, u32[]{:S(2)}) copy-start(bf16[4,4,128,128]{3,2,1,0:T(8,128)(2,1)} %param.19) | copy-start | bytes 1572868
  1.6 15.7 %collective-permute-start.1 = (bf16[16,8,128]{2,0,1:T(8,128)(2,1)S(1)}, bf16[16,8,128]{2,0,1:T(8,128)(2,1)S(1)}, u32[]{:S(2)}, u32[]{:S(2)}) collective-permute-start(bf16[16,8,128]{2,0,1:T(8,128)(2,1)S(1)} %pad_maximum_fusion.3), channel_id=1, source_target_pairs={{0,1},{1,2},{2,3},{3,4},{4,5},{5,6},{6,7},{7,8},{8,9},{9,10},{10,1... | collective-permute-start | bytes 98312 | tf_op jit(solution)/shard_map/ppermute | solution.py:17
  6.8 10.5 %collective-permute-start.2 = (bf16[16,8,128]{2,0,1:T(8,128)(2,1)S(1)}, bf16[16,8,128]{2,0,1:T(8,128)(2,1)S(1)}, u32[]{:S(2)}, u32[]{:S(2)}) collective-permute-start(bf16[16,8,128]{2,0,1:T(8,128)(2,1)S(1)} %pad_maximum_fusion.3), channel_id=1, source_target_pairs={{1,0},{2,1},{3,2},{4,3},{5,4},{6,5},{7,6},{8,7},{9,8},{10,9},{11,1... | collective-permute-start | bytes 98312 | tf_op jit(solution)/shard_map/ppermute | solution.py:17
  8.7 8.6 %collective-permute-start = (bf16[12,8,128]{2,0,1:T(8,128)(2,1)S(1)}, bf16[12,8,128]{2,0,1:T(8,128)(2,1)S(1)}, u32[]{:S(2)}, u32[]{:S(2)}) collective-permute-start(bf16[12,8,128]{2,0,1:T(8,128)(2,1)S(1)} %copy.35), channel_id=1, source_target_pairs={{0,2},{1,3},{2,4},{3,5},{4,6},{5,7},{6,8},{7,9},{8,10},{9,11},{10,... | collective-permute-start | bytes 73736 | tf_op jit(solution)/shard_map/ppermute | solution.py:17
  11.6 6.8 %collective-permute-start.3 = (bf16[12,8,128]{2,0,1:T(8,128)(2,1)S(1)}, bf16[12,8,128]{2,0,1:T(8,128)(2,1)S(1)}, u32[]{:S(2)}, u32[]{:S(2)}) collective-permute-start(bf16[12,8,128]{2,0,1:T(8,128)(2,1)S(1)} %copy.35), channel_id=1, source_target_pairs={{2,0},{3,1},{4,2},{5,3},{6,4},{7,5},{8,6},{9,7},{10,8},{11,9},{12,... | collective-permute-start | bytes 73736 | tf_op jit(solution)/shard_map/ppermute | solution.py:17
  21.8 1.0 %copy-start.3 = (bf16[3,3,128,128]{3,2,1,0:T(8,128)(2,1)S(1)}, bf16[3,3,128,128]{3,2,1,0:T(8,128)(2,1)}, u32[]{:S(2)}) copy-start(bf16[3,3,128,128]{3,2,1,0:T(8,128)(2,1)} %param.17) | copy-start | bytes 884740
  21.8 1.0 %copy-start.10 = (pred[8,9]{0,1:T(8,128)(4,1)S(1)}, pred[8,9]{0,1:T(8,128)(4,1)}, u32[]{:S(2)}) copy-start(pred[8,9]{0,1:T(8,128)(4,1)} %constant.184) | copy-start | bytes 220
  22.8 1.1 %copy-start.4 = (bf16[3,3,128,128]{3,2,1,0:T(8,128)(2,1)S(1)}, bf16[3,3,128,128]{3,2,1,0:T(8,128)(2,1)}, u32[]{:S(2)}) copy-start(bf16[3,3,128,128]{3,2,1,0:T(8,128)(2,1)} %param.18) | copy-start | bytes 884740
  27.6 1.0 %copy-start.5 = (bf16[3,3,128,128]{3,2,1,0:T(8,128)(2,1)S(1)}, bf16[3,3,128,128]{3,2,1,0:T(8,128)(2,1)}, u32[]{:S(2)}) copy-start(bf16[3,3,128,128]{3,2,1,0:T(8,128)(2,1)} %param.20) | copy-start | bytes 884740
  27.6 1.0 %copy-start.9 = (pred[8,17]{0,1:T(8,128)(4,1)S(1)}, pred[8,17]{0,1:T(8,128)(4,1)}, u32[]{:S(2)}) copy-start(pred[8,17]{0,1:T(8,128)(4,1)} %constant.183) | copy-start | bytes 412
  35.0 1.0 %copy-start.6 = (bf16[3,3,128,128]{3,2,1,0:T(8,128)(2,1)S(1)}, bf16[3,3,128,128]{3,2,1,0:T(8,128)(2,1)}, u32[]{:S(2)}) copy-start(bf16[3,3,128,128]{3,2,1,0:T(8,128)(2,1)} %param.23) | copy-start | bytes 884740
  35.9 1.0 %copy-start.7 = (bf16[3,3,128,128]{3,2,1,0:T(8,128)(2,1)S(1)}, bf16[3,3,128,128]{3,2,1,0:T(8,128)(2,1)}, u32[]{:S(2)}) copy-start(bf16[3,3,128,128]{3,2,1,0:T(8,128)(2,1)} %param.24) | copy-start | bytes 884740
  36.9 1.0 %copy-start.2 = (bf16[4,4,128,128]{3,2,1,0:T(8,128)(2,1)S(1)}, bf16[4,4,128,128]{3,2,1,0:T(8,128)(2,1)}, u32[]{:S(2)}) copy-start(bf16[4,4,128,128]{3,2,1,0:T(8,128)(2,1)} %param.25) | copy-start | bytes 1572868
  38.8 1.0 %copy-start.8 = (bf16[3,3,128,128]{3,2,1,0:T(8,128)(2,1)S(1)}, bf16[3,3,128,128]{3,2,1,0:T(8,128)(2,1)}, u32[]{:S(2)}) copy-start(bf16[3,3,128,128]{3,2,1,0:T(8,128)(2,1)} %param.26) | copy-start | bytes 884740
  40.8 0.7 %copy-start.1 = (f32[1,4,8,128]{3,2,1,0:T(8,128)S(1)}, f32[1,4,8,128]{3,2,1,0:T(8,128)}, u32[]{:S(2)}) copy-start(f32[1,4,8,128]{3,2,1,0:T(8,128)} %param.15) | copy-start | bytes 49156
  41.7 9.6 %collective-permute-start.4 = (bf16[4,8,128]{2,0,1:T(4,128)(2,1)S(1)}, bf16[4,8,128]{2,0,1:T(4,128)(2,1)S(1)}, u32[]{:S(2)}, u32[]{:S(2)}) collective-permute-start(bf16[4,8,128]{2,0,1:T(4,128)(2,1)S(1)} %get-tuple-element.5), channel_id=1, source_target_pairs={{0,1},{1,2},{2,3},{3,4},{4,5},{5,6},{6,7},{7,8},{8,9},{9,10},{10,1... | collective-permute-start | bytes 24584 | tf_op jit(solution)/shard_map/ppermute | solution.py:17
  49.1 7.1 %collective-permute-start.5 = (bf16[4,8,128]{2,0,1:T(4,128)(2,1)S(1)}, bf16[4,8,128]{2,0,1:T(4,128)(2,1)S(1)}, u32[]{:S(2)}, u32[]{:S(2)}) collective-permute-start(bf16[4,8,128]{2,0,1:T(4,128)(2,1)S(1)} %get-tuple-element.5), channel_id=1, source_target_pairs={{1,0},{2,1},{3,2},{4,3},{5,4},{6,5},{7,6},{8,7},{9,8},{10,9},{11,1... | collective-permute-start | bytes 24584 | tf_op jit(solution)/shard_map/ppermute | solution.py:17

commit v4 on v3

--- a/solution.py
+++ b/solution.py
@@ -173,14 +173,17 @@
     noise_in = (gains[0][0] * residual_field).astype(jnp.bfloat16)
     near = jnp.concatenate([noise_in, conditioning], axis=0)
     if rows == dif_halo:
-        near_below = from_tile(near, -1)
-        near_above = from_tile(near, 1)
+        cols = conditioning.shape[2]
+        cond_flat = conditioning.reshape(-1, cols)
+        near_flat = jnp.concatenate([noise_in.reshape(-1, cols), cond_flat], axis=0)
+        near_below = from_tile(near_flat, -1).reshape(near.shape)
+        near_above = from_tile(near_flat, 1).reshape(near.shape)
         near_wide = jnp.concatenate([near_below, near, near_above], axis=1)
         cond_wide = jnp.concatenate(
             [
-                from_tile(conditioning, -2),
+                from_tile(cond_flat, -2).reshape(conditioning.shape),
                 near_wide[noise_count:],
-                from_tile(conditioning, 2),
+                from_tile(cond_flat, 2).reshape(conditioning.shape),
             ],
             axis=1,
         )

time: 65 us -> 66.6 us (1.025)
  other arithmetic: 2.55 us -> 4.05 us
  waiting for transfers between devices: 5.91 us -> 4.93 us
  starting transfers between devices: 22.1 us -> 23 us
    ppermute x6, waiting for transfers between devices: 5.91 us -> 4.93 us  [from_tile(): return lax.ppermute(values, 'tile', pairs)]
    ppermute x6, starting transfers between devices: 22.1 us -> 23 us  [from_tile(): return lax.ppermute(values, 'tile', pairs)]
    convert_element_type x1 -> x2, other arithmetic: 0.72 us -> 1.51 us  [shards(): noise_in = (gains[0][0] * residual_field).astype(jnp.bfloat16)]
    concatenate x2, other arithmetic: 0.19 us -> 0.91 us  [the longest x1 0.74 us: shards(): near_flat = jnp.concatenate([noise_in.reshape(-1, cols), cond_flat], axis=0)]
  transfers between devices with their start and end apart: 6 -> 6, of which waited for: 2 -> 1; matrix products, arithmetic and copies ran while one was open for 5% -> 7% of each run, Pallas kernels for 0% -> 0%
where the time goes in v4:
time: 66.6 us; the launch traced here: 65.8 us
  starting transfers between devices  23 us (35%)
  local copies, waits for them, and re-layouts  17 us (26%)
  matrix products  15.7 us (24%)
  waiting for transfers between devices  4.93 us (7%)
  other arithmetic  4.05 us (6%)
  between operations  1.02 us (2%)
    ppermute x6, starting transfers between devices, from_tile(): return lax.ppermute(values, 'tile', pairs)  23 us
    conv_general_dilated x12, matrix products, conv(): lax.conv_general_dilated(lhs, rhs, window_strides=strides, padding=paddin...  11.1 us
    unnamed x51, local copies, waits for them, and re-layouts  8.51 us
    ppermute x6, waiting for transfers between devices, from_tile(): return lax.ppermute(values, 'tile', pairs)  4.93 us
    dot_general x3, matrix products, conv_in(): jnp.einsum('krw,ko->rwo', patches, flat, preferred_element_type=jnp.float32)  3.14 us
    conv_general_dilated x17, local copies, waits for them, and re-layouts, conv(): lax.conv_general_dilated(lhs, rhs, window_strides=strides, padding=paddin...  2.34 us
    pad x2, local copies, waits for them, and re-layouts, conv_in(): weight = jnp.pad(weight, ((0, 0), (0, 0), (0, extra), (0, 0)))  1.61 us
    convert_element_type x2, other arithmetic, shards(): noise_in = (gains[0][0] * residual_field).astype(jnp.bfloat16)  1.51 us
  transfers between devices with their start and end apart: 6, of which 1 were waited for; matrix products, arithmetic and copies ran while one was open for 7% of the time, Pallas kernels for 0%

profile of v4, /device:TPU:415, one launch (start us, length us, event | category | flops | bytes accessed | tf_op | source)
XLA Modules:
  0.0 65.8 jit_solution(3615018003493663194)
XLA Ops:
  0.0 0.8 %fusion.248 = bf16[32,128]{1,0:T(8,128)(2,1)S(1)} fusion(f32[1,4,8,128]{3,2,1,0:T(8,128)} %param.15), kind=kLoop, calls=%fused_computation.300 | loop fusion | flops 8192 | bytes 24576 | tf_op jit(solution)/shard_map/convert_element_type | solution.py:173
  0.8 0.7 %pad_maximum_fusion.3 = bf16[128,128]{1,0:T(8,128)(2,1)S(1)} fusion(bf16[96,128]{1,0:T(8,128)(2,1)} %bitcast.207, bf16[32,128]{1,0:T(8,128)(2,1)S(1)} %fusion.248), kind=kLoop, calls=%fused_computation.272 | loop fusion | flops 65536 | bytes 65536 | tf_op jit(solution)/shard_map/concatenate | solution.py:178
  1.5 5.2 %collective-permute-start.1 = (bf16[128,128]{1,0:T(8,128)(2,1)S(1)}, bf16[128,128]{1,0:T(8,128)(2,1)S(1)}, u32[]{:S(2)}, u32[]{:S(2)}) collective-permute-start(bf16[128,128]{1,0:T(8,128)(2,1)S(1)} %pad_maximum_fusion.3), channel_id=1, source_target_pairs={{0,1},{1,2},{2,3},{3,4},{4,5},{5,6},{6,7},{7,8},{8,9},{9,10},{10,1... | collective-permute-start | bytes 98312 | tf_op jit(solution)/shard_map/ppermute | solution.py:17
  6.8 1.9 %collective-permute-start.2 = (bf16[128,128]{1,0:T(8,128)(2,1)S(1)}, bf16[128,128]{1,0:T(8,128)(2,1)S(1)}, u32[]{:S(2)}, u32[]{:S(2)}) collective-permute-start(bf16[128,128]{1,0:T(8,128)(2,1)S(1)} %pad_maximum_fusion.3), channel_id=1, source_target_pairs={{1,0},{2,1},{3,2},{4,3},{5,4},{6,5},{7,6},{8,7},{9,8},{10,9},{11,1... | collective-permute-start | bytes 98312 | tf_op jit(solution)/shard_map/ppermute | solution.py:17
  8.7 2.8 %collective-permute-start = (bf16[96,128]{1,0:T(8,128)(2,1)}, bf16[96,128]{1,0:T(8,128)(2,1)S(1)}, u32[]{:S(2)}, u32[]{:S(2)}) collective-permute-start(bf16[96,128]{1,0:T(8,128)(2,1)} %bitcast.208), channel_id=1, source_target_pairs={{0,2},{1,3},{2,4},{3,5},{4,6},{5,7},{6,8},{7,9},{8,10},{9,11},{10,... | collective-permute-start | bytes 73736 | tf_op jit(solution)/shard_map/ppermute | solution.py:17
  11.5 2.5 %collective-permute-start.3 = (bf16[96,128]{1,0:T(8,128)(2,1)}, bf16[96,128]{1,0:T(8,128)(2,1)S(1)}, u32[]{:S(2)}, u32[]{:S(2)}) collective-permute-start(bf16[96,128]{1,0:T(8,128)(2,1)} %bitcast.209), channel_id=1, source_target_pairs={{2,0},{3,1},{4,2},{5,3},{6,4},{7,5},{8,6},{9,7},{10,8},{11,9},{12,... | collective-permute-start | bytes 73736 | tf_op jit(solution)/shard_map/ppermute | solution.py:17
  14.0 0.7 %fusion.245 = bf16[4,8,128]{2,0,1:T(4,128)(2,1)S(1)} fusion(f32[1,4,8,128]{3,2,1,0:T(8,128)} %param.15), kind=kLoop, calls=%fused_computation.295 | loop fusion | flops 8192 | bytes 24576 | tf_op jit(solution)/shard_map/convert_element_type | solution.py:173
  14.9 0.7 %copy.34 = bf16[12,8,128]{2,0,1:T(8,128)(2,1)S(1)} copy(bf16[12,8,128]{2,1,0:T(8,128)(2,1)} %param.14) | data formatting | bytes 49152 | tf_op args[0]
  15.7 0.7 %reshape.294 = bf16[36,128,1]{1,0,2:T(8,128)(2,1)S(1)} reshape(bf16[3,3,4,128]{3,2,1,0:T(4,128)(2,1)} %param.21) | data formatting | bytes 18432 | tf_op jit(solution)/shard_map/reshape | solution.py:120
  16.4 0.8 %pad.32 = bf16[3,3,16,128]{3,2,1,0:T(8,128)(2,1)S(1)} pad(bf16[3,3,12,128]{3,2,1,0:T(8,128)(2,1)} %param.16, bf16[]{:T(256)} %constant.42.clone.1), padding=0_0x0_0x0_4x0_0 | pad | bytes 64514 | tf_op jit(solution)/shard_map/jit(_pad)/pad | solution.py:80
  17.2 0.8 %pad.35 = bf16[3,3,32,128]{3,2,1,0:T(8,128)(2,1)S(1)} pad(bf16[3,3,20,128]{3,2,1,0:T(8,128)(2,1)} %param.22, bf16[]{:T(256)} %constant.42.clone.1), padding=0_0x0_0x0_12x0_0 | pad | bytes 119810 | tf_op jit(solution)/shard_map/jit(_pad)/pad | solution.py:80
  18.0 0.7 %reshape.296 = bf16[36,128,1]{1,0,2:T(8,128)(2,1)S(1)} reshape(bf16[3,3,4,128]{3,2,1,0:T(4,128)(2,1)} %param.27) | data formatting | bytes 18432 | tf_op jit(solution)/shard_map/reshape | solution.py:120
  18.8 0.2 fusion.154
  20.0 1.3 %select_convert_fusion = bf16[37,128,128]{2,1,0:T(8,128)(2,1)S(1)} fusion(bf16[144,37,128]{2,0,1:T(8,128)(2,1)S(1)} %slice_dynamic-update-slice_fusion.18, bf16[144,128,1]{1,0,2:T(8,128)(2,1)S(1)} %bitcast.212, pred[37]{0:T(512)(128)(4,1)S(1)} %compare_and_fusion.7), kind=kOutput, calls=%fused_computation.2 | convolution fusion | flops 178225152 | bytes 2613285 | tf_op jit(solution)/shard_map/krw,ko->rwo/dot_general | solution.py:88
  21.3 0.8 %copy.79 = bf16[37,1,128,128]{3,0,2,1:T(8,128)(2,1)S(1)} copy(bf16[37,1,128,128]{3,2,0,1:T(8,128)(2,1)S(1)} %bitcast.193) | data formatting | bytes 2424832
  22.1 0.2 pad.39.clone
  22.4 0.4 copy.41
  22.8 0.5 copy-done.3
  23.3 1.0 %fusion.59 = bf16[18,1,8,9,128]{4,2,3,0,1:T(8,128)(2,1)S(1)} fusion(bf16[3,3,128,128]{3,2,1,0:T(8,128)(2,1)S(1)} %copy-done.3, bf16[37,1,7,2,128]{4,2,3,0,1:T(8,128)(2,1)S(1)} %slice.297, bf16[37,1,8,18,128]{4,2,3,0,1:T(8,128)(2,1)S(1)} %copy.41, pred[18]{0:T(512)(128)(4,1)S(1)} %compare_and_fusion.5, pred[8,9]{0,1:T(8,128)(4,1)S(1)} %copy-done.10), kind=kOutput, calls=%fused_computation.96 | convolution fusion | flops 388079616 | bytes 2123354 | tf_op jit(solution)/shard_map/conv_general_dilated | solution.py:52
  24.4 0.9 %fusion.94 = bf16[16,8,9,128]{3,1,2,0:T(8,128)(2,1)S(1)} fusion(bf16[3,3,128,128]{3,2,1,0:T(8,128)(2,1)S(1)} %copy-done.4, bf16[18,1,7,1,128]{4,2,3,0,1:T(8,128)(2,1)S(1)} %get-tuple-element.10, bf16[18,1,7,1,128]{4,2,3,0,1:T(8,128)(2,1)S(1)} %get-tuple-element.9, bf16[18,1,8,9,128]{4,2,3,0,1:T(8,128)(2,1)S(1)} %fusion.59, ...), kind=kOutput, calls=%fused_computation.130 | convolution fusion | flops 342798336 | bytes 986200 | tf_op jit(solution)/shard_map/conv_general_dilated | solution.py:52
  25.5 1.1 %fusion.139 = f32[28,8,16,128]{3,1,2,0:T(8,128)S(1)} fusion(bf16[4,4,128,128]{3,2,1,0:T(8,128)(2,1)S(1)} %copy-done, bf16[16,1,7,1,128]{4,2,3,0,1:T(8,128)(2,1)S(1)} %get-tuple-element.12, bf16[16,1,7,1,128]{4,2,3,0,1:T(8,128)(2,1)S(1)} %get-tuple-element.11, bf16[16,1,8,8,128]{4,2,3,0,1:T(8,128)(2,1)S(1)} %copy.44), kind=kOutput, calls=%fused_computation.162 | convolution fusion | flops 471400448 | bytes 2678784 | tf_op jit(solution)/shard_map/conv_general_dilated | solution.py:52
  26.6 0.3 copy.47
  27.0 0.3 fusion.3
  27.3 0.6 copy.80
  27.9 0.2 pad.45.clone
  28.1 0.4 copy.50
  28.5 0.5 copy-done.5
  29.1 2.4 %select_convert_fusion.1 = bf16[26,8,17,128]{3,1,2,0:T(8,128)(2,1)S(1)} fusion(bf16[3,3,128,128]{3,2,1,0:T(8,128)(2,1)S(1)} %copy-done.5, bf16[28,1,7,2,128]{4,2,3,0,1:T(8,128)(2,1)S(1)} %slice.303, bf16[28,1,8,17,128]{4,2,3,0,1:T(8,128)(2,1)S(1)} %copy.50, pred[26]{0:T(512)(128)(4,1)S(1)} %compare_and_fusion.9, pred[8,17]{0,1:T(8,128)(4,1)S(1)} %copy-done.9), kind=kOutput, calls=%fused_computation.14 | convolution fusion | flops 1049245696 | bytes 2275490 | tf_op jit(solution)/shard_map/conv_general_dilated | solution.py:52
  31.5 0.2 copy.51
  31.8 0.8 %convolution_bitcast_fusion = f32[36,26,128]{2,0,1:T(8,128)S(1)} fusion(bf16[36,128,1]{1,0,2:T(8,128)(2,1)S(1)} %reshape.294, bf16[26,1,128,128]{3,0,2,1:T(8,128)(2,1)S(1)} %slice.304), kind=kOutput, calls=%fused_computation.29 | convolution fusion | flops 30670848 | bytes 1340416 | tf_op jit(solution)/shard_map/tc,rwc->trw/dot_general | solution.py:121
  32.6 0.2 fusion.291
  32.9 0.2 fusion.107
  33.1 0.1 slice_dynamic-update-slice_fusion.16
  33.3 0.1 slice_dynamic-update-slice_fusion.15
  34.1 0.9 %select_convert_fusion.3 = bf16[21,128,128]{2,1,0:T(8,128)(2,1)S(1)} fusion(bf16[288,21,128]{2,0,1:T(8,128)(2,1)S(1)} %slice_dynamic-update-slice_fusion.9, bf16[288,128,1]{1,0,2:T(8,128)(2,1)S(1)} %bitcast.210, pred[21]{0:T(512)(128)(4,1)S(1)} %compare_and_fusion.2), kind=kOutput, calls=%fused_computation.25 | convolution fusion | flops 200245248 | bytes 2310165 | tf_op jit(solution)/shard_map/krw,ko->rwo/dot_general | solution.py:88
  35.0 0.5 copy.81
  35.5 0.2 pad.47.clone
  35.7 0.2 copy.55
  35.9 0.5 copy-done.6
  36.5 0.6 fusion.134
  37.1 0.3 copy-done.7
  37.4 0.5 fusion.166
  38.1 0.4 copy-done.2
  38.5 0.6 fusion.195
  39.5 0.2 reshape.210
  39.7 0.6 copy-done.8
  40.3 1.0 %select_convert_fusion.5 = bf16[10,8,17,128]{3,1,2,0:T(8,128)(2,1)S(1)} fusion(bf16[3,3,128,128]{3,2,1,0:T(8,128)(2,1)S(1)} %copy-done.8, bf16[12,1,7,2,128]{4,2,3,0,1:T(8,128)(2,1)S(1)} %slice.325, bf16[12,1,8,17,128]{4,2,3,0,1:T(8,128)(2,1)S(1)} %copy.63, pred[10]{0:T(512)(128)(4,1)S(1)} %compare_and_fusion.4, pred[8,17]{0,1:T(8,128)(4,1)S(1)} %copy-done.9), kind=kOutput, calls=%fused_computation.93 | convolution fusion | flops 403699712 | bytes 1104018 | tf_op jit(solution)/shard_map/conv_general_dilated | solution.py:52
  41.6 0.3 convolution_bitcast_fusion.2
  42.2 8.4 %collective-permute-start.4 = (bf16[4,8,128]{2,0,1:T(4,128)(2,1)S(1)}, bf16[4,8,128]{2,0,1:T(4,128)(2,1)S(1)}, u32[]{:S(2)}, u32[]{:S(2)}) collective-permute-start(bf16[4,8,128]{2,0,1:T(4,128)(2,1)S(1)} %get-tuple-element.5), channel_id=1, source_target_pairs={{0,1},{1,2},{2,3},{3,4},{4,5},{5,6},{6,7},{7,8},{8,9},{9,10},{10,1... | collective-permute-start | bytes 24584 | tf_op jit(solution)/shard_map/ppermute | solution.py:17
  50.6 2.1 %collective-permute-start.5 = (bf16[4,8,128]{2,0,1:T(4,128)(2,1)S(1)}, bf16[4,8,128]{2,0,1:T(4,128)(2,1)S(1)}, u32[]{:S(2)}, u32[]{:S(2)}) collective-permute-start(bf16[4,8,128]{2,0,1:T(4,128)(2,1)S(1)} %get-tuple-element.5), channel_id=1, source_target_pairs={{1,0},{2,1},{3,2},{4,3},{5,4},{6,5},{7,6},{8,7},{9,8},{10,9},{11,1... | collective-permute-start | bytes 24584 | tf_op jit(solution)/shard_map/ppermute | solution.py:17
  52.8 4.9 %collective-permute-done.5 = bf16[4,8,128]{2,0,1:T(4,128)(2,1)S(1)} collective-permute-done((bf16[4,8,128]{2,0,1:T(4,128)(2,1)S(1)}, bf16[4,8,128]{2,0,1:T(4,128)(2,1)S(1)}, u32[]{:S(2)}, u32[]{:S(2)}) %collective-permute-start.5) | collective-permute-done | bytes 8224 | tf_op jit(solution)/shard_map/ppermute | solution.py:17
  57.7 0.3 fusion.117
  58.9 0.1 slice_dynamic-update-slice_fusion
  59.0 0.9 %select_convert_fusion.2 = bf16[21,128,128]{2,1,0:T(8,128)(2,1)S(1)} fusion(bf16[288,21,128]{2,0,1:T(8,128)(2,1)S(1)} %slice_dynamic-update-slice_fusion, bf16[288,128,1]{1,0,2:T(8,128)(2,1)S(1)} %bitcast.211, pred[21]{0:T(512)(128)(4,1)S(1)} %compare_and_fusion.2), kind=kOutput, calls=%fused_computation.24 | convolution fusion | flops 200245248 | bytes 2310165 | tf_op jit(solution)/shard_map/krw,ko->rwo/dot_general | solution.py:88
  59.9 0.5 copy.82
  60.4 0.2 pad.55.clone
  60.6 0.2 copy.67
  60.8 0.7 fusion.126
  61.5 0.6 fusion.176
  62.2 0.6 fusion.200
  63.2 0.2 reshape.234
  63.4 1.0 %select_convert_fusion.4 = bf16[10,8,17,128]{3,1,2,0:T(8,128)(2,1)S(1)} fusion(bf16[3,3,128,128]{3,2,1,0:T(8,128)(2,1)S(1)} %copy-done.8, bf16[12,1,7,2,128]{4,2,3,0,1:T(8,128)(2,1)S(1)} %slice.346, bf16[12,1,8,17,128]{4,2,3,0,1:T(8,128)(2,1)S(1)} %copy.75, pred[10]{0:T(512)(128)(4,1)S(1)} %compare_and_fusion.4, pred[8,17]{0,1:T(8,128)(4,1)S(1)} %copy-done.9), kind=kOutput, calls=%fused_computation.92 | convolution fusion | flops 403699712 | bytes 1104018 | tf_op jit(solution)/shard_map/conv_general_dilated | solution.py:52
  64.7 0.3 convolution_bitcast_fusion.1
  65.2 0.6 copy.77
  (100 shorter events, 5.0 us)
Async XLA Ops:
  0.0 25.5 %copy-start = (bf16[4,4,128,128]{3,2,1,0:T(8,128)(2,1)S(1)}, bf16[4,4,128,128]{3,2,1,0:T(8,128)(2,1)}, u32[]{:S(2)}) copy-start(bf16[4,4,128,128]{3,2,1,0:T(8,128)(2,1)} %param.19) | copy-start | bytes 1572868
  1.5 17.2 %collective-permute-start.1 = (bf16[128,128]{1,0:T(8,128)(2,1)S(1)}, bf16[128,128]{1,0:T(8,128)(2,1)S(1)}, u32[]{:S(2)}, u32[]{:S(2)}) collective-permute-start(bf16[128,128]{1,0:T(8,128)(2,1)S(1)} %pad_maximum_fusion.3), channel_id=1, source_target_pairs={{0,1},{1,2},{2,3},{3,4},{4,5},{5,6},{6,7},{7,8},{8,9},{9,10},{10,1... | collective-permute-start | bytes 98312 | tf_op jit(solution)/shard_map/ppermute | solution.py:17
  6.8 12.0 %collective-permute-start.2 = (bf16[128,128]{1,0:T(8,128)(2,1)S(1)}, bf16[128,128]{1,0:T(8,128)(2,1)S(1)}, u32[]{:S(2)}, u32[]{:S(2)}) collective-permute-start(bf16[128,128]{1,0:T(8,128)(2,1)S(1)} %pad_maximum_fusion.3), channel_id=1, source_target_pairs={{1,0},{2,1},{3,2},{4,3},{5,4},{6,5},{7,6},{8,7},{9,8},{10,9},{11,1... | collective-permute-start | bytes 98312 | tf_op jit(solution)/shard_map/ppermute | solution.py:17
  8.7 10.0 %collective-permute-start = (bf16[96,128]{1,0:T(8,128)(2,1)}, bf16[96,128]{1,0:T(8,128)(2,1)S(1)}, u32[]{:S(2)}, u32[]{:S(2)}) collective-permute-start(bf16[96,128]{1,0:T(8,128)(2,1)} %bitcast.208), channel_id=1, source_target_pairs={{0,2},{1,3},{2,4},{3,5},{4,6},{5,7},{6,8},{7,9},{8,10},{9,11},{10,... | collective-permute-start | bytes 73736 | tf_op jit(solution)/shard_map/ppermute | solution.py:17
  11.5 7.2 %collective-permute-start.3 = (bf16[96,128]{1,0:T(8,128)(2,1)}, bf16[96,128]{1,0:T(8,128)(2,1)S(1)}, u32[]{:S(2)}, u32[]{:S(2)}) collective-permute-start(bf16[96,128]{1,0:T(8,128)(2,1)} %bitcast.209), channel_id=1, source_target_pairs={{2,0},{3,1},{4,2},{5,3},{6,4},{7,5},{8,6},{9,7},{10,8},{11,9},{12,... | collective-permute-start | bytes 73736 | tf_op jit(solution)/shard_map/ppermute | solution.py:17
  22.3 1.0 %copy-start.3 = (bf16[3,3,128,128]{3,2,1,0:T(8,128)(2,1)S(1)}, bf16[3,3,128,128]{3,2,1,0:T(8,128)(2,1)}, u32[]{:S(2)}) copy-start(bf16[3,3,128,128]{3,2,1,0:T(8,128)(2,1)} %param.17) | copy-start | bytes 884740
  22.4 1.0 %copy-start.10 = (pred[8,9]{0,1:T(8,128)(4,1)S(1)}, pred[8,9]{0,1:T(8,128)(4,1)}, u32[]{:S(2)}) copy-start(pred[8,9]{0,1:T(8,128)(4,1)} %constant.184) | copy-start | bytes 220
  23.3 1.1 %copy-start.4 = (bf16[3,3,128,128]{3,2,1,0:T(8,128)(2,1)S(1)}, bf16[3,3,128,128]{3,2,1,0:T(8,128)(2,1)}, u32[]{:S(2)}) copy-start(bf16[3,3,128,128]{3,2,1,0:T(8,128)(2,1)} %param.18) | copy-start | bytes 884740
  28.1 1.0 %copy-start.5 = (bf16[3,3,128,128]{3,2,1,0:T(8,128)(2,1)S(1)}, bf16[3,3,128,128]{3,2,1,0:T(8,128)(2,1)}, u32[]{:S(2)}) copy-start(bf16[3,3,128,128]{3,2,1,0:T(8,128)(2,1)} %param.20) | copy-start | bytes 884740
  28.1 1.0 %copy-start.9 = (pred[8,17]{0,1:T(8,128)(4,1)S(1)}, pred[8,17]{0,1:T(8,128)(4,1)}, u32[]{:S(2)}) copy-start(pred[8,17]{0,1:T(8,128)(4,1)} %constant.183) | copy-start | bytes 412
  35.5 1.0 %copy-start.6 = (bf16[3,3,128,128]{3,2,1,0:T(8,128)(2,1)S(1)}, bf16[3,3,128,128]{3,2,1,0:T(8,128)(2,1)}, u32[]{:S(2)}) copy-start(bf16[3,3,128,128]{3,2,1,0:T(8,128)(2,1)} %param.23) | copy-start | bytes 884740
  36.5 1.0 %copy-start.7 = (bf16[3,3,128,128]{3,2,1,0:T(8,128)(2,1)S(1)}, bf16[3,3,128,128]{3,2,1,0:T(8,128)(2,1)}, u32[]{:S(2)}) copy-start(bf16[3,3,128,128]{3,2,1,0:T(8,128)(2,1)} %param.24) | copy-start | bytes 884740
  37.4 1.0 %copy-start.2 = (bf16[4,4,128,128]{3,2,1,0:T(8,128)(2,1)S(1)}, bf16[4,4,128,128]{3,2,1,0:T(8,128)(2,1)}, u32[]{:S(2)}) copy-start(bf16[4,4,128,128]{3,2,1,0:T(8,128)(2,1)} %param.25) | copy-start | bytes 1572868
  39.3 1.0 %copy-start.8 = (bf16[3,3,128,128]{3,2,1,0:T(8,128)(2,1)S(1)}, bf16[3,3,128,128]{3,2,1,0:T(8,128)(2,1)}, u32[]{:S(2)}) copy-start(bf16[3,3,128,128]{3,2,1,0:T(8,128)(2,1)} %param.26) | copy-start | bytes 884740
  41.3 0.7 %copy-start.1 = (f32[1,4,8,128]{3,2,1,0:T(8,128)S(1)}, f32[1,4,8,128]{3,2,1,0:T(8,128)}, u32[]{:S(2)}) copy-start(f32[1,4,8,128]{3,2,1,0:T(8,128)} %param.15) | copy-start | bytes 49156
  42.2 10.6 %collective-permute-start.4 = (bf16[4,8,128]{2,0,1:T(4,128)(2,1)S(1)}, bf16[4,8,128]{2,0,1:T(4,128)(2,1)S(1)}, u32[]{:S(2)}, u32[]{:S(2)}) collective-permute-start(bf16[4,8,128]{2,0,1:T(4,128)(2,1)S(1)} %get-tuple-element.5), channel_id=1, source_target_pairs={{0,1},{1,2},{2,3},{3,4},{4,5},{5,6},{6,7},{7,8},{8,9},{9,10},{10,1... | collective-permute-start | bytes 24584 | tf_op jit(solution)/shard_map/ppermute | solution.py:17
  50.6 7.1 %collective-permute-start.5 = (bf16[4,8,128]{2,0,1:T(4,128)(2,1)S(1)}, bf16[4,8,128]{2,0,1:T(4,128)(2,1)S(1)}, u32[]{:S(2)}, u32[]{:S(2)}) collective-permute-start(bf16[4,8,128]{2,0,1:T(4,128)(2,1)S(1)} %get-tuple-element.5), channel_id=1, source_target_pairs={{1,0},{2,1},{3,2},{4,3},{5,4},{6,5},{7,6},{8,7},{9,8},{10,9},{11,1... | collective-permute-start | bytes 24584 | tf_op jit(solution)/shard_map/ppermute | solution.py:17

commit v5 on v3

--- a/solution.py
+++ b/solution.py
@@ -195,6 +195,8 @@
     reg_mean = mean_wide[:, dif_halo : dif_halo + rows]
 
     fixed_in = jnp.concatenate([cond_near, mean_input], axis=0)
+    dif_first = jnp.concatenate([dif_in[:, :, noise_count:], dif_in[:, :, :noise_count]], axis=2)
+    dif_order = (dif_first,) + tuple(dif_weights[1:])
     field_in = near_wide[:noise_count]
     for step_index in range(STEPS):
         in_gain, skip_gain, out_gain, step_gain = gains[step_index]
@@ -202,8 +204,8 @@
             field_in = halo_rows(
                 (in_gain * residual_field).astype(jnp.bfloat16), 1, dif_halo, dif_halo
             )
-        inputs = jnp.concatenate([field_in, fixed_in], axis=0)
-        network = unet(inputs, -dif_halo, 0, rows, dif_weights, base, grid_rows)
+        inputs = jnp.concatenate([fixed_in, field_in], axis=0)
+        network = unet(inputs, -dif_halo, 0, rows, dif_order, base, grid_rows)
         denoised = skip_gain * residual_field + out_gain * network
         residual_field = residual_field + step_gain * (residual_field - denoised)
     return (reg_mean + residual_field)[None]

time: 65 us -> 65.5 us (level)
  waiting for transfers between devices: 5.91 us -> 5.15 us
  starting transfers between devices: 22.1 us -> 22.8 us
    slice x0 -> x3, local copies, waits for them, and re-layouts: none -> 1.59 us  [the longest x1 0.83 us: shards(): dif_in[:, :, noise_count:]]
    pad x2 -> x1, local copies, waits for them, and re-layouts: 1.61 us -> 0.78 us  [conv_in(): weight = jnp.pad(weight, ((0, 0), (0, 0), (0, extra), (0, 0)))]
    ppermute x6, waiting for transfers between devices: 5.91 us -> 5.15 us  [from_tile(): return lax.ppermute(values, 'tile', pairs)]
    ppermute x6, starting transfers between devices: 22.1 us -> 22.8 us  [from_tile(): return lax.ppermute(values, 'tile', pairs)]
  transfers between devices with their start and end apart: 6 -> 6, of which waited for: 2 -> 2; matrix products, arithmetic and copies ran while one was open for 5% -> 6% of each run, Pallas kernels for 0% -> 0%
where the time goes in v5:
time: 65.5 us; the launch traced here: 64.7 us
  starting transfers between devices  22.8 us (35%)
  local copies, waits for them, and re-layouts  17.7 us (27%)
  matrix products  15.7 us (24%)
  waiting for transfers between devices  5.15 us (8%)
  other arithmetic  2.4 us (4%)
  between operations  0.97 us (1%)
    ppermute x6, starting transfers between devices, from_tile(): return lax.ppermute(values, 'tile', pairs)  22.8 us
    conv_general_dilated x12, matrix products, conv(): lax.conv_general_dilated(lhs, rhs, window_strides=strides, padding=paddin...  11.1 us
    unnamed x51, local copies, waits for them, and re-layouts  8.45 us
    ppermute x6, waiting for transfers between devices, from_tile(): return lax.ppermute(values, 'tile', pairs)  5.15 us
    dot_general x3, matrix products, conv_in(): jnp.einsum('krw,ko->rwo', patches, flat, preferred_element_type=jnp.float32)  3.15 us
    conv_general_dilated x17, local copies, waits for them, and re-layouts, conv(): lax.conv_general_dilated(lhs, rhs, window_strides=strides, padding=paddin...  2.34 us
    dot_general x3, matrix products, conv_out(): jnp.einsum('tc,rwc->trw', flat, refined, preferred_element_type=jnp.float32)  1.5 us
    reshape x2, local copies, waits for them, and re-layouts, conv_out(): flat = weight.reshape(9 * outs, weight.shape[3])  1.44 us
  transfers between devices with their start and end apart: 6, of which 2 were waited for; matrix products, arithmetic and copies ran while one was open for 6% of the time, Pallas kernels for 0%

profile of v5, /device:TPU:415, one launch (start us, length us, event | category | flops | bytes accessed | tf_op | source)
XLA Modules:
  0.0 64.7 jit_solution(8287103704116413590)
XLA Ops:
  0.0 0.8 %copy.35 = bf16[12,8,128]{2,0,1:T(8,128)(2,1)S(1)} copy(bf16[12,8,128]{2,1,0:T(8,128)(2,1)} %param.14) | data formatting | bytes 49152 | tf_op args[0]
  0.8 0.7 %fusion.247 = bf16[4,8,128]{2,0,1:T(4,128)(2,1)S(1)} fusion(f32[1,4,8,128]{3,2,1,0:T(8,128)} %param.15), kind=kLoop, calls=%fused_computation.301 | loop fusion | flops 8192 | bytes 24576 | tf_op jit(solution)/shard_map/convert_element_type | solution.py:173
  1.6 5.2 %collective-permute-start.1 = (bf16[16,8,128]{2,0,1:T(8,128)(2,1)S(1)}, bf16[16,8,128]{2,0,1:T(8,128)(2,1)S(1)}, u32[]{:S(2)}, u32[]{:S(2)}) collective-permute-start(bf16[16,8,128]{2,0,1:T(8,128)(2,1)S(1)} %pad_maximum_fusion.4), channel_id=1, source_target_pairs={{0,1},{1,2},{2,3},{3,4},{4,5},{5,6},{6,7},{7,8},{8,9},{9,10},{10,1... | collective-permute-start | bytes 98312 | tf_op jit(solution)/shard_map/ppermute | solution.py:17
  6.8 1.9 %collective-permute-start.2 = (bf16[16,8,128]{2,0,1:T(8,128)(2,1)S(1)}, bf16[16,8,128]{2,0,1:T(8,128)(2,1)S(1)}, u32[]{:S(2)}, u32[]{:S(2)}) collective-permute-start(bf16[16,8,128]{2,0,1:T(8,128)(2,1)S(1)} %pad_maximum_fusion.4), channel_id=1, source_target_pairs={{1,0},{2,1},{3,2},{4,3},{5,4},{6,5},{7,6},{8,7},{9,8},{10,9},{11,1... | collective-permute-start | bytes 98312 | tf_op jit(solution)/shard_map/ppermute | solution.py:17
  8.7 2.8 %collective-permute-start = (bf16[12,8,128]{2,0,1:T(8,128)(2,1)S(1)}, bf16[12,8,128]{2,0,1:T(8,128)(2,1)S(1)}, u32[]{:S(2)}, u32[]{:S(2)}) collective-permute-start(bf16[12,8,128]{2,0,1:T(8,128)(2,1)S(1)} %copy.35), channel_id=1, source_target_pairs={{0,2},{1,3},{2,4},{3,5},{4,6},{5,7},{6,8},{7,9},{8,10},{9,11},{10,... | collective-permute-start | bytes 73736 | tf_op jit(solution)/shard_map/ppermute | solution.py:17
  11.6 2.5 %collective-permute-start.3 = (bf16[12,8,128]{2,0,1:T(8,128)(2,1)S(1)}, bf16[12,8,128]{2,0,1:T(8,128)(2,1)S(1)}, u32[]{:S(2)}, u32[]{:S(2)}) collective-permute-start(bf16[12,8,128]{2,0,1:T(8,128)(2,1)S(1)} %copy.35), channel_id=1, source_target_pairs={{2,0},{3,1},{4,2},{5,3},{6,4},{7,5},{8,6},{9,7},{10,8},{11,9},{12,... | collective-permute-start | bytes 73736 | tf_op jit(solution)/shard_map/ppermute | solution.py:17
  14.0 0.8 %slice.238 = bf16[3,3,16,128]{3,2,1,0:T(8,128)(2,1)S(1)} slice(bf16[3,3,20,128]{3,2,1,0:T(8,128)(2,1)} %param.22), slice={[0:3], [0:3], [4:20], [0:128]} | slice | bytes 73728 | tf_op jit(solution)/shard_map/slice | solution.py:198
  14.9 0.7 %slice.239 = bf16[3,3,4,128]{3,2,1,0:T(4,128)(2,1)S(1)} slice(bf16[3,3,20,128]{3,2,1,0:T(8,128)(2,1)} %param.22), slice={[0:3], [0:3], [0:4], [0:128]} | slice | bytes 18432 | tf_op jit(solution)/shard_map/slice | solution.py:198
  15.8 0.7 %reshape.269 = bf16[36,128,1]{1,0,2:T(8,128)(2,1)S(1)} reshape(bf16[3,3,4,128]{3,2,1,0:T(4,128)(2,1)} %param.21) | data formatting | bytes 18432 | tf_op jit(solution)/shard_map/reshape | solution.py:120
  16.5 0.7 %reshape.271 = bf16[36,128,1]{1,0,2:T(8,128)(2,1)S(1)} reshape(bf16[3,3,4,128]{3,2,1,0:T(4,128)(2,1)} %param.27) | data formatting | bytes 18432 | tf_op jit(solution)/shard_map/reshape | solution.py:120
  17.2 0.8 %pad.32 = bf16[3,3,16,128]{3,2,1,0:T(8,128)(2,1)S(1)} pad(bf16[3,3,12,128]{3,2,1,0:T(8,128)(2,1)} %param.16, bf16[]{:T(256)} %constant.42.clone.1), padding=0_0x0_0x0_4x0_0 | pad | bytes 64514 | tf_op jit(solution)/shard_map/jit(_pad)/pad | solution.py:80
  18.1 0.2 collective-permute-done.3
  18.3 0.2 fusion.142
  19.5 1.3 %select_convert_fusion = bf16[37,128,128]{2,1,0:T(8,128)(2,1)S(1)} fusion(bf16[144,37,128]{2,0,1:T(8,128)(2,1)S(1)} %slice_dynamic-update-slice_fusion.9, bf16[144,128,1]{1,0,2:T(8,128)(2,1)S(1)} %bitcast.202, pred[37]{0:T(512)(128)(4,1)S(1)} %compare_and_fusion.7), kind=kOutput, calls=%fused_computation.2 | convolution fusion | flops 178225152 | bytes 2613285 | tf_op jit(solution)/shard_map/krw,ko->rwo/dot_general | solution.py:88
  20.8 0.8 %copy.79 = bf16[37,1,128,128]{3,0,2,1:T(8,128)(2,1)S(1)} copy(bf16[37,1,128,128]{3,2,0,1:T(8,128)(2,1)S(1)} %bitcast.186) | data formatting | bytes 2424832
  21.6 0.2 pad.39.clone
  21.9 0.4 copy.41
  22.3 0.5 copy-done.3
  22.8 1.0 %fusion.55 = bf16[18,1,8,9,128]{4,2,3,0,1:T(8,128)(2,1)S(1)} fusion(bf16[3,3,128,128]{3,2,1,0:T(8,128)(2,1)S(1)} %copy-done.3, bf16[37,1,7,2,128]{4,2,3,0,1:T(8,128)(2,1)S(1)} %slice.308, bf16[37,1,8,18,128]{4,2,3,0,1:T(8,128)(2,1)S(1)} %copy.41, pred[18]{0:T(512)(128)(4,1)S(1)} %compare_and_fusion.5, pred[8,9]{0,1:T(8,128)(4,1)S(1)} %copy-done.10), kind=kOutput, calls=%fused_computation.101 | convolution fusion | flops 388079616 | bytes 2123354 | tf_op jit(solution)/shard_map/conv_general_dilated | solution.py:52
  23.9 0.9 %fusion.90 = bf16[16,8,9,128]{3,1,2,0:T(8,128)(2,1)S(1)} fusion(bf16[3,3,128,128]{3,2,1,0:T(8,128)(2,1)S(1)} %copy-done.4, bf16[18,1,7,1,128]{4,2,3,0,1:T(8,128)(2,1)S(1)} %get-tuple-element.10, bf16[18,1,7,1,128]{4,2,3,0,1:T(8,128)(2,1)S(1)} %get-tuple-element.9, bf16[18,1,8,9,128]{4,2,3,0,1:T(8,128)(2,1)S(1)} %fusion.55, ...), kind=kOutput, calls=%fused_computation.135 | convolution fusion | flops 342798336 | bytes 986200 | tf_op jit(solution)/shard_map/conv_general_dilated | solution.py:52
  25.0 1.1 %fusion.127 = f32[28,8,16,128]{3,1,2,0:T(8,128)S(1)} fusion(bf16[4,4,128,128]{3,2,1,0:T(8,128)(2,1)S(1)} %copy-done, bf16[16,1,7,1,128]{4,2,3,0,1:T(8,128)(2,1)S(1)} %get-tuple-element.12, bf16[16,1,7,1,128]{4,2,3,0,1:T(8,128)(2,1)S(1)} %get-tuple-element.11, bf16[16,1,8,8,128]{4,2,3,0,1:T(8,128)(2,1)S(1)} %copy.44), kind=kOutput, calls=%fused_computation.159 | convolution fusion | flops 471400448 | bytes 2678784 | tf_op jit(solution)/shard_map/conv_general_dilated | solution.py:52
  26.1 0.3 copy.47
  26.5 0.3 fusion.3
  26.8 0.6 copy.80
  27.4 0.2 pad.45.clone
  27.6 0.4 copy.50
  28.0 0.5 copy-done.5
  28.5 2.4 %select_convert_fusion.1 = bf16[26,8,17,128]{3,1,2,0:T(8,128)(2,1)S(1)} fusion(bf16[3,3,128,128]{3,2,1,0:T(8,128)(2,1)S(1)} %copy-done.5, bf16[28,1,7,2,128]{4,2,3,0,1:T(8,128)(2,1)S(1)} %slice.314, bf16[28,1,8,17,128]{4,2,3,0,1:T(8,128)(2,1)S(1)} %copy.50, pred[26]{0:T(512)(128)(4,1)S(1)} %compare_and_fusion.9, pred[8,17]{0,1:T(8,128)(4,1)S(1)} %copy-done.9), kind=kOutput, calls=%fused_computation.14 | convolution fusion | flops 1049245696 | bytes 2275490 | tf_op jit(solution)/shard_map/conv_general_dilated | solution.py:52
  31.0 0.2 copy.51
  31.3 0.8 %convolution_bitcast_fusion = f32[36,26,128]{2,0,1:T(8,128)S(1)} fusion(bf16[36,128,1]{1,0,2:T(8,128)(2,1)S(1)} %reshape.269, bf16[26,1,128,128]{3,0,2,1:T(8,128)(2,1)S(1)} %slice.315), kind=kOutput, calls=%fused_computation.29 | convolution fusion | flops 30670848 | bytes 1340416 | tf_op jit(solution)/shard_map/tc,rwc->trw/dot_general | solution.py:121
  32.1 0.2 fusion.292
  33.3 0.9 %select_convert_fusion.3 = bf16[21,128,128]{2,1,0:T(8,128)(2,1)S(1)} fusion(bf16[288,21,128]{2,0,1:T(8,128)(2,1)S(1)} %fusion.188, bf16[288,128,1]{1,0,2:T(8,128)(2,1)S(1)} %bitcast.200, pred[21]{0:T(512)(128)(4,1)S(1)} %compare_and_fusion.2), kind=kOutput, calls=%fused_computation.25 | convolution fusion | flops 200245248 | bytes 2310165 | tf_op jit(solution)/shard_map/krw,ko->rwo/dot_general | solution.py:88
  34.2 0.5 copy.81
  34.7 0.2 pad.47.clone
  34.9 0.2 copy.55
  35.1 0.5 copy-done.6
  35.7 0.6 fusion.122
  36.3 0.3 copy-done.7
  36.6 0.5 fusion.154
  37.3 0.4 copy-done.2
  37.7 0.6 fusion.192
  38.7 0.2 reshape.185
  38.9 0.6 copy-done.8
  39.5 1.0 %select_convert_fusion.5 = bf16[10,8,17,128]{3,1,2,0:T(8,128)(2,1)S(1)} fusion(bf16[3,3,128,128]{3,2,1,0:T(8,128)(2,1)S(1)} %copy-done.8, bf16[12,1,7,2,128]{4,2,3,0,1:T(8,128)(2,1)S(1)} %slice.329, bf16[12,1,8,17,128]{4,2,3,0,1:T(8,128)(2,1)S(1)} %copy.63, pred[10]{0:T(512)(128)(4,1)S(1)} %compare_and_fusion.4, pred[8,17]{0,1:T(8,128)(4,1)S(1)} %copy-done.9), kind=kOutput, calls=%fused_computation.98 | convolution fusion | flops 403699712 | bytes 1104018 | tf_op jit(solution)/shard_map/conv_general_dilated | solution.py:52
  40.8 0.3 convolution_bitcast_fusion.2
  41.4 8.2 %collective-permute-start.4 = (bf16[4,8,128]{2,0,1:T(4,128)(2,1)S(1)}, bf16[4,8,128]{2,0,1:T(4,128)(2,1)S(1)}, u32[]{:S(2)}, u32[]{:S(2)}) collective-permute-start(bf16[4,8,128]{2,0,1:T(4,128)(2,1)S(1)} %get-tuple-element.5), channel_id=1, source_target_pairs={{0,1},{1,2},{2,3},{3,4},{4,5},{5,6},{6,7},{7,8},{8,9},{9,10},{10,1... | collective-permute-start | bytes 24584 | tf_op jit(solution)/shard_map/ppermute | solution.py:17
  49.6 2.1 %collective-permute-start.5 = (bf16[4,8,128]{2,0,1:T(4,128)(2,1)S(1)}, bf16[4,8,128]{2,0,1:T(4,128)(2,1)S(1)}, u32[]{:S(2)}, u32[]{:S(2)}) collective-permute-start(bf16[4,8,128]{2,0,1:T(4,128)(2,1)S(1)} %get-tuple-element.5), channel_id=1, source_target_pairs={{1,0},{2,1},{3,2},{4,3},{5,4},{6,5},{7,6},{8,7},{9,8},{10,9},{11,1... | collective-permute-start | bytes 24584 | tf_op jit(solution)/shard_map/ppermute | solution.py:17
  51.8 4.9 %collective-permute-done.5 = bf16[4,8,128]{2,0,1:T(4,128)(2,1)S(1)} collective-permute-done((bf16[4,8,128]{2,0,1:T(4,128)(2,1)S(1)}, bf16[4,8,128]{2,0,1:T(4,128)(2,1)S(1)}, u32[]{:S(2)}, u32[]{:S(2)}) %collective-permute-start.5) | collective-permute-done | bytes 8224 | tf_op jit(solution)/shard_map/ppermute | solution.py:17
  56.7 0.2 fusion.102
  57.0 0.1 slice_dynamic-update-slice_fusion.7
  57.1 0.1 slice_dynamic-update-slice_fusion.6
  57.5 0.1 slice_dynamic-update-slice_fusion.3
  57.7 0.1 slice_dynamic-update-slice_fusion.1
  58.0 0.9 %select_convert_fusion.2 = bf16[21,128,128]{2,1,0:T(8,128)(2,1)S(1)} fusion(bf16[288,21,128]{2,0,1:T(8,128)(2,1)S(1)} %slice_dynamic-update-slice_fusion, bf16[288,128,1]{1,0,2:T(8,128)(2,1)S(1)} %bitcast.201, pred[21]{0:T(512)(128)(4,1)S(1)} %compare_and_fusion.2), kind=kOutput, calls=%fused_computation.24 | convolution fusion | flops 200245248 | bytes 2310165 | tf_op jit(solution)/shard_map/krw,ko->rwo/dot_general | solution.py:88
  58.9 0.5 copy.82
  59.4 0.2 pad.55.clone
  59.5 0.2 copy.67
  59.8 0.6 %fusion.114 = bf16[10,1,8,9,128]{4,2,3,0,1:T(8,128)(2,1)S(1)} fusion(bf16[3,3,128,128]{3,2,1,0:T(8,128)(2,1)S(1)} %copy-done.6, bf16[21,1,7,2,128]{4,2,3,0,1:T(8,128)(2,1)S(1)} %slice.344, bf16[21,1,8,18,128]{4,2,3,0,1:T(8,128)(2,1)S(1)} %copy.67, pred[10]{0:T(512)(128)(4,1)S(1)} %compare_and_fusion, pred[8,9]{0,1:T(8,128)(4,1)S(1)} %copy-done.10), kind=kOutput, calls=%fused_computation.153 | convolution fusion | flops 215654400 | bytes 1328722 | tf_op jit(solution)/shard_map/conv_general_dilated | solution.py:52
  60.5 0.6 fusion.164
  61.1 0.6 fusion.197
  62.1 0.2 reshape.209
  62.4 1.0 %select_convert_fusion.4 = bf16[10,8,17,128]{3,1,2,0:T(8,128)(2,1)S(1)} fusion(bf16[3,3,128,128]{3,2,1,0:T(8,128)(2,1)S(1)} %copy-done.8, bf16[12,1,7,2,128]{4,2,3,0,1:T(8,128)(2,1)S(1)} %slice.350, bf16[12,1,8,17,128]{4,2,3,0,1:T(8,128)(2,1)S(1)} %copy.75, pred[10]{0:T(512)(128)(4,1)S(1)} %compare_and_fusion.4, pred[8,17]{0,1:T(8,128)(4,1)S(1)} %copy-done.9), kind=kOutput, calls=%fused_computation.97 | convolution fusion | flops 403699712 | bytes 1104018 | tf_op jit(solution)/shard_map/conv_general_dilated | solution.py:52
  63.7 0.3 convolution_bitcast_fusion.1
  64.1 0.6 copy.77
  (98 shorter events, 4.8 us)
Async XLA Ops:
  0.0 25.0 %copy-start = (bf16[4,4,128,128]{3,2,1,0:T(8,128)(2,1)S(1)}, bf16[4,4,128,128]{3,2,1,0:T(8,128)(2,1)}, u32[]{:S(2)}) copy-start(bf16[4,4,128,128]{3,2,1,0:T(8,128)(2,1)} %param.19) | copy-start | bytes 1572868
  1.6 16.5 %collective-permute-start.1 = (bf16[16,8,128]{2,0,1:T(8,128)(2,1)S(1)}, bf16[16,8,128]{2,0,1:T(8,128)(2,1)S(1)}, u32[]{:S(2)}, u32[]{:S(2)}) collective-permute-start(bf16[16,8,128]{2,0,1:T(8,128)(2,1)S(1)} %pad_maximum_fusion.4), channel_id=1, source_target_pairs={{0,1},{1,2},{2,3},{3,4},{4,5},{5,6},{6,7},{7,8},{8,9},{9,10},{10,1... | collective-permute-start | bytes 98312 | tf_op jit(solution)/shard_map/ppermute | solution.py:17
  6.8 11.2 %collective-permute-start.2 = (bf16[16,8,128]{2,0,1:T(8,128)(2,1)S(1)}, bf16[16,8,128]{2,0,1:T(8,128)(2,1)S(1)}, u32[]{:S(2)}, u32[]{:S(2)}) collective-permute-start(bf16[16,8,128]{2,0,1:T(8,128)(2,1)S(1)} %pad_maximum_fusion.4), channel_id=1, source_target_pairs={{1,0},{2,1},{3,2},{4,3},{5,4},{6,5},{7,6},{8,7},{9,8},{10,9},{11,1... | collective-permute-start | bytes 98312 | tf_op jit(solution)/shard_map/ppermute | solution.py:17
  8.7 9.4 %collective-permute-start = (bf16[12,8,128]{2,0,1:T(8,128)(2,1)S(1)}, bf16[12,8,128]{2,0,1:T(8,128)(2,1)S(1)}, u32[]{:S(2)}, u32[]{:S(2)}) collective-permute-start(bf16[12,8,128]{2,0,1:T(8,128)(2,1)S(1)} %copy.35), channel_id=1, source_target_pairs={{0,2},{1,3},{2,4},{3,5},{4,6},{5,7},{6,8},{7,9},{8,10},{9,11},{10,... | collective-permute-start | bytes 73736 | tf_op jit(solution)/shard_map/ppermute | solution.py:17
  11.6 6.8 %collective-permute-start.3 = (bf16[12,8,128]{2,0,1:T(8,128)(2,1)S(1)}, bf16[12,8,128]{2,0,1:T(8,128)(2,1)S(1)}, u32[]{:S(2)}, u32[]{:S(2)}) collective-permute-start(bf16[12,8,128]{2,0,1:T(8,128)(2,1)S(1)} %copy.35), channel_id=1, source_target_pairs={{2,0},{3,1},{4,2},{5,3},{6,4},{7,5},{8,6},{9,7},{10,8},{11,9},{12,... | collective-permute-start | bytes 73736 | tf_op jit(solution)/shard_map/ppermute | solution.py:17
  21.8 1.0 %copy-start.3 = (bf16[3,3,128,128]{3,2,1,0:T(8,128)(2,1)S(1)}, bf16[3,3,128,128]{3,2,1,0:T(8,128)(2,1)}, u32[]{:S(2)}) copy-start(bf16[3,3,128,128]{3,2,1,0:T(8,128)(2,1)} %param.17) | copy-start | bytes 884740
  21.8 1.0 %copy-start.10 = (pred[8,9]{0,1:T(8,128)(4,1)S(1)}, pred[8,9]{0,1:T(8,128)(4,1)}, u32[]{:S(2)}) copy-start(pred[8,9]{0,1:T(8,128)(4,1)} %constant.184) | copy-start | bytes 220
  22.8 1.1 %copy-start.4 = (bf16[3,3,128,128]{3,2,1,0:T(8,128)(2,1)S(1)}, bf16[3,3,128,128]{3,2,1,0:T(8,128)(2,1)}, u32[]{:S(2)}) copy-start(bf16[3,3,128,128]{3,2,1,0:T(8,128)(2,1)} %param.18) | copy-start | bytes 884740
  27.6 1.0 %copy-start.5 = (bf16[3,3,128,128]{3,2,1,0:T(8,128)(2,1)S(1)}, bf16[3,3,128,128]{3,2,1,0:T(8,128)(2,1)}, u32[]{:S(2)}) copy-start(bf16[3,3,128,128]{3,2,1,0:T(8,128)(2,1)} %param.20) | copy-start | bytes 884740
  27.6 1.0 %copy-start.9 = (pred[8,17]{0,1:T(8,128)(4,1)S(1)}, pred[8,17]{0,1:T(8,128)(4,1)}, u32[]{:S(2)}) copy-start(pred[8,17]{0,1:T(8,128)(4,1)} %constant.183) | copy-start | bytes 412
  34.7 1.0 %copy-start.6 = (bf16[3,3,128,128]{3,2,1,0:T(8,128)(2,1)S(1)}, bf16[3,3,128,128]{3,2,1,0:T(8,128)(2,1)}, u32[]{:S(2)}) copy-start(bf16[3,3,128,128]{3,2,1,0:T(8,128)(2,1)} %param.23) | copy-start | bytes 884740
  35.7 1.0 %copy-start.7 = (bf16[3,3,128,128]{3,2,1,0:T(8,128)(2,1)S(1)}, bf16[3,3,128,128]{3,2,1,0:T(8,128)(2,1)}, u32[]{:S(2)}) copy-start(bf16[3,3,128,128]{3,2,1,0:T(8,128)(2,1)} %param.24) | copy-start | bytes 884740
  36.6 1.0 %copy-start.2 = (bf16[4,4,128,128]{3,2,1,0:T(8,128)(2,1)S(1)}, bf16[4,4,128,128]{3,2,1,0:T(8,128)(2,1)}, u32[]{:S(2)}) copy-start(bf16[4,4,128,128]{3,2,1,0:T(8,128)(2,1)} %param.25) | copy-start | bytes 1572868
  38.5 1.0 %copy-start.8 = (bf16[3,3,128,128]{3,2,1,0:T(8,128)(2,1)S(1)}, bf16[3,3,128,128]{3,2,1,0:T(8,128)(2,1)}, u32[]{:S(2)}) copy-start(bf16[3,3,128,128]{3,2,1,0:T(8,128)(2,1)} %param.26) | copy-start | bytes 884740
  40.5 0.7 %copy-start.1 = (f32[1,4,8,128]{3,2,1,0:T(8,128)S(1)}, f32[1,4,8,128]{3,2,1,0:T(8,128)}, u32[]{:S(2)}) copy-start(f32[1,4,8,128]{3,2,1,0:T(8,128)} %param.15) | copy-start | bytes 49156
  41.4 10.4 %collective-permute-start.4 = (bf16[4,8,128]{2,0,1:T(4,128)(2,1)S(1)}, bf16[4,8,128]{2,0,1:T(4,128)(2,1)S(1)}, u32[]{:S(2)}, u32[]{:S(2)}) collective-permute-start(bf16[4,8,128]{2,0,1:T(4,128)(2,1)S(1)} %get-tuple-element.5), channel_id=1, source_target_pairs={{0,1},{1,2},{2,3},{3,4},{4,5},{5,6},{6,7},{7,8},{8,9},{9,10},{10,1... | collective-permute-start | bytes 24584 | tf_op jit(solution)/shard_map/ppermute | solution.py:17
  49.6 7.1 %collective-permute-start.5 = (bf16[4,8,128]{2,0,1:T(4,128)(2,1)S(1)}, bf16[4,8,128]{2,0,1:T(4,128)(2,1)S(1)}, u32[]{:S(2)}, u32[]{:S(2)}) collective-permute-start(bf16[4,8,128]{2,0,1:T(4,128)(2,1)S(1)} %get-tuple-element.5), channel_id=1, source_target_pairs={{1,0},{2,1},{3,2},{4,3},{5,4},{6,5},{7,6},{8,7},{9,8},{10,9},{11,1... | collective-permute-start | bytes 24584 | tf_op jit(solution)/shard_map/ppermute | solution.py:17
